TPU v7x, 256 devices: a whole 4x4x8 slice. The times are simulated.
256 devices in a mesh: row: 32 (over z, y_hi, core), col: 8 (over x, y_lo).
Axes of the slice: x: 4, y: 4 (y_hi: 2, y_lo: 2; y = y_hi * 2 + y_lo), z: 8, core: 2. Of those that a mesh axis runs over, the one named last changes fastest.
Arguments:
- affinity_tiles: bfloat16 [1024, 512, 512], P(('row', 'col')), may hold values from -6 to 6
- tile_rows: int32 [1024], P(('row', 'col')), may hold values from -1 to 63, as said below
- tile_cols: int32 [1024], P(('row', 'col')), may hold values from -1 to 63, as said below
- lang_counts: int32 [32], replicated, may hold values from 1 to 8192, 32768 in all
- start_basis: float32 [8, 4096, 64], P('col', 'row'), may hold values from -6 to 6
Outputs:
- eigen_basis: float32 [8, 4096, 64], P('col', 'row')
Inputs may be any that keep to these rules, and one draw needn't show every extreme that they name: `tile_rows`: the slots of device (r, c) are entries (r * 8 + c) * 4 onward of both lists. Every used slot names a distinct block with block row from r * 2 to (r + 1) * 2 - 1, block column from c * 8 to (c + 1) * 8 - 1, and block row <= block column; no block is named twice. Empty slots hold -1 in both lists and come after the used slots of their device. Device (0, 7) uses all 4 slots. `tile_cols`: same slots as tile_rows.
All inputs are finite; a program needn't handle non-finite values.
Results may differ from a plain program's by a relative error of at most 0.0044.
Values may be sent and summed in bfloat16 or wider, within the bound.
No kernel may reach another device: no remote copies, remote signals or barrier semaphores. Data moves between devices by JAX's collectives and lax.ppermute only.
A program may use at most 64 MiB of HBM per device.

v0:
```python
import jax
import jax.numpy as jnp
from jax import lax
from jax.sharding import PartitionSpec as P

ROW_BLOCKS = 2
ITERS = 3


highest = lax.Precision.HIGHEST


def broadcast(value, axis, root):
    mine = lax.axis_index(axis) == root
    return lax.psum(jnp.where(mine, value, jnp.zeros_like(value)), axis)


def add_block(target, addend, offset):
    current = lax.dynamic_slice_in_dim(target, offset, addend.shape[0], 0)
    return lax.dynamic_update_slice_in_dim(target, current + addend, offset, 0)


def membership(first_doc, doc_count, lang_ends, lang_starts):
    doc_index = first_doc + jnp.arange(doc_count, dtype=jnp.int32)
    return (
        (doc_index[:, None] >= lang_starts[None, :]) & (doc_index[:, None] < lang_ends[None, :])
    ).astype(jnp.float32)


def apply_tiles(affinity_tiles, pick_rows, pick_cols, scaled_rows, scaled_cols, col_blocks):
    slot_count, tile_size, _ = affinity_tiles.shape
    vectors = scaled_cols.shape[1]
    blocks_r = scaled_rows.reshape(ROW_BLOCKS, tile_size, vectors)
    blocks_c = scaled_cols.reshape(col_blocks, tile_size, vectors)
    chosen_c = jnp.einsum(
        "tq,qjk->tjk", pick_cols, blocks_c, preferred_element_type=jnp.float32
    ).astype(jnp.bfloat16)
    chosen_r = jnp.einsum(
        "tp,pik->tik", pick_rows, blocks_r, preferred_element_type=jnp.float32
    ).astype(jnp.bfloat16)
    forward = jnp.einsum(
        "tij,tjk->tik", affinity_tiles, chosen_c, preferred_element_type=jnp.float32
    )
    backward = jnp.einsum(
        "tij,tik->tjk", affinity_tiles, chosen_r, preferred_element_type=jnp.float32
    )
    part_rows = jnp.einsum("tp,tik->pik", pick_rows.astype(jnp.float32), forward, precision=highest)
    part_cols = jnp.einsum(
        "tq,tjk->qjk", pick_cols.astype(jnp.float32), backward, precision=highest
    )
    return (
        part_rows.reshape(ROW_BLOCKS * tile_size, vectors),
        part_cols.reshape(col_blocks * tile_size, vectors),
    )


def shards(affinity_tiles, tile_rows, tile_cols, lang_counts, start_basis):
    row_devices = lax.axis_size("row")
    col_devices = lax.axis_size("col")
    group_ratio = row_devices // col_devices
    col_blocks = ROW_BLOCKS * row_devices // col_devices
    tile_size = affinity_tiles.shape[1]
    row_span = ROW_BLOCKS * tile_size
    col_span = col_blocks * tile_size
    piece_rows = start_basis.shape[1]
    doc_total = piece_rows * row_devices * col_devices
    my_row = lax.axis_index("row")
    my_col = lax.axis_index("col")
    is_owner = (my_row // group_ratio == my_col).astype(jnp.float32)
    offset = my_row % group_ratio * row_span
    piece_offset = my_row * piece_rows
    present = tile_rows >= 0
    local_p = tile_rows - my_row * ROW_BLOCKS
    local_q = tile_cols - my_col * col_blocks
    pick_rows = (
        (local_p[:, None] == jnp.arange(ROW_BLOCKS, dtype=jnp.int32)[None, :]) & present[:, None]
    ).astype(jnp.bfloat16)
    pick_cols = (
        (local_q[:, None] == jnp.arange(col_blocks, dtype=jnp.int32)[None, :]) & present[:, None]
    ).astype(jnp.bfloat16)
    magnitude = jnp.abs(affinity_tiles)
    row_mass = jnp.sum(magnitude, axis=2, dtype=jnp.float32)
    col_mass = jnp.sum(magnitude, axis=1, dtype=jnp.float32)
    degree_rows = jnp.einsum(
        "tp,ti->pi", pick_rows.astype(jnp.float32), row_mass, precision=highest
    ).reshape(row_span)
    degree_cols = jnp.einsum(
        "tq,tj->qj", pick_cols.astype(jnp.float32), col_mass, precision=highest
    ).reshape(col_span)
    rows_degree = lax.psum(degree_rows, "col")
    degree_cols = add_block(degree_cols, is_owner * rows_degree, offset)
    inv_own = lax.rsqrt(1.0 + lax.psum_scatter(degree_cols, "row", scatter_dimension=0, tiled=True))
    prior_scale = lax.psum(jnp.sum(inv_own), ("row", "col")) / doc_total
    lang_ends = jnp.cumsum(lang_counts)
    lang_starts = lang_ends - lang_counts
    counts_real = lang_counts.astype(jnp.float32)
    member_own = membership(my_col * col_span + piece_offset, piece_rows, lang_ends, lang_starts)
    basis_own = start_basis[0]
    for iteration in range(ITERS):
        lang_now = lax.psum(jnp.dot(member_own.T, basis_own, precision=highest), ("row", "col"))
        lang_mean = prior_scale * (lang_now / counts_real[:, None])
        scaled_cols = lax.all_gather(
            (inv_own[:, None] * basis_own).astype(jnp.bfloat16), "row", axis=0, tiled=True
        )
        scaled_rows = broadcast(
            lax.dynamic_slice_in_dim(scaled_cols, offset, row_span, 0), "col", my_row // group_ratio
        )
        part_rows, part_cols = apply_tiles(
            affinity_tiles, pick_rows, pick_cols, scaled_rows, scaled_cols, col_blocks
        )
        rows_sum = lax.psum(part_rows, "col")
        part_cols = add_block(part_cols, is_owner * rows_sum, offset)
        product_own = lax.psum_scatter(part_cols, "row", scatter_dimension=0, tiled=True)
        applied_own = inv_own[:, None] * product_own + jnp.dot(
            member_own, lang_mean, precision=highest
        )
        gram_part = jnp.dot(applied_own.T, applied_own, precision=highest)
        gram_matrix = lax.psum(gram_part, ("row", "col"))
        factor = jnp.linalg.cholesky(gram_matrix / doc_total)
        basis_own = jax.scipy.linalg.solve_triangular(factor, applied_own.T, lower=True).T
    return basis_own[None]


def solution(mesh):
    in_specs = (
        P(("row", "col"), None, None),
        P(("row", "col")),
        P(("row", "col")),
        P(),
        P("col", "row", None),
    )
    out_specs = P("col", "row", None)
    return jax.shard_map(shards, mesh=mesh, in_specs=in_specs, out_specs=out_specs, check_vma=False)
```

profile of v0, /device:TPU:6, one launch (start us, length us, event | category | flops | bytes accessed | tf_op | source)
XLA Modules:
  0.0 1383.7 jit_solution(9308302912916534671)
XLA Ops:
  6.5 0.7 broadcast_compare_fusion
  7.2 0.7 broadcast_subtract_fusion
  7.9 0.7 broadcast_subtract_fusion.1
  8.6 2.2 convert_reduce_fusion
  11.0 16.5 %psum.98 = f32[1024]{0:T(1024)S(1)} all-reduce(f32[1024]{0:T(1024)S(1)} %bitcast.181), channel_id=1, replica_groups=mesh['row'=32,'col'=8] {'col'}, use_global_device_ids=true, to_apply=%region_2.3 | all-reduce | flops 1024 | bytes 8192 | tf_op jit(solution)/shard_map/psum | solution.py:90
  27.7 132.3 %all-reduce = f32[4096]{0:T(1024)S(1)} all-reduce(f32[4096]{0:T(1024)S(1)} %add_dynamic-update-slice_fusion.3), channel_id=2, replica_groups=mesh['row'=32,'col'=8] {'row'}, use_global_device_ids=true, to_apply=%region_3.4.clone | all-reduce | flops 4096 | bytes 32768
  161.2 0.7 fusion.72
  161.9 37.8 %all_gather.9 = bf16[4096,64]{0,1:T(8,128)(2,1)S(1)} all-gather(bf16[128,64]{0,1:T(8,128)(2,1)S(1)} %fusion.39), channel_id=1, replica_groups=mesh['row'=32,'col'=8] {'row'}, dimensions={0}, use_global_device_ids=true | all-gather | bytes 540672 | tf_op jit(solution)/shard_map/all_gather | solution.py:102
  199.7 0.7 reshape.85
  201.0 0.7 convolution_bitcast_fusion.4
  201.8 0.9 fusion.8
  202.7 0.7 copy.46
  203.5 74.9 %all-reduce.9.cloned.1.call-done = bf16[2,512,64]{1,0,2:T(2,128)(2,1)} async-done(((bf16[2,512,64]{1,0,2:T(2,128)(2,1)}), bf16[2,512,64]{1,0,2:T(2,128)(2,1)}) %all-reduce.9.cloned.1.call-update) | async-done | bytes 131088 | tf_op jit(solution)/shard_map/psum | solution.py:15
  278.4 1.2 convolution_convert_fusion.5
  280.1 1.0 fusion.10
  281.7 77.9 %all-reduce.11.cloned.1.call-done = f32[1024,64]{0,1:T(8,128)} async-done(((f32[1024,64]{0,1:T(8,128)}), f32[1024,64]{0,1:T(8,128)}) %all-reduce.11.cloned.1.call-update) | async-done | bytes 262160 | tf_op jit(solution)/shard_map/psum | solution.py:111
  359.6 1.0 add_dynamic-update-slice_fusion.2
  360.7 1.0 copy-done.2
  362.2 75.7 %all-reduce.1 = (f32[32,64]{1,0:T(8,128)S(1)}, f32[]{:T(128)}) all-reduce(f32[32,64]{1,0:T(8,128)S(1)} %fusion.22, f32[]{:T(128)} %get-tuple-element.11), channel_id=1, replica_groups=mesh['row'=32,'col'=8] {'row','col'}, use_global_device_ids=true, to_apply=%region_10.11 | all-reduce | flops 2049 | bytes 16392 | tf_op jit(solution)/shard_map/psum | solution.py:100
  438.6 42.0 %reduce-scatter.4.cloned.1.call-done = f32[128,64]{0,1:T(8,128)} async-done(((f32[4096,64]{0,1:T(8,128)}), f32[128,64]{0,1:T(8,128)}) %reduce-scatter.4.cloned.1.call-update) | async-done | bytes 32784 | tf_op jit(solution)/shard_map/reduce_scatter | solution.py:113
  480.6 1.1 convolution_add_fusion.2
  481.8 73.3 %psum.103 = f32[64,64]{0,1:T(8,128)S(1)} all-reduce(f32[64,64]{0,1:T(8,128)S(1)} %fusion.75), channel_id=1, replica_groups=mesh['row'=32,'col'=8] {'row','col'}, use_global_device_ids=true, to_apply=%region_11.12 | all-reduce | flops 4096 | bytes 32768 | tf_op jit(solution)/shard_map/psum | solution.py:118
  555.2 5.8 cholesky.59
  561.1 0.6 compare_reduce_fusion.2
  561.7 0.7 fusion.24
  562.4 4.9 custom-call.7
  567.6 39.5 %all_gather.10 = bf16[4096,64]{0,1:T(8,128)(2,1)S(1)} all-gather(bf16[128,64]{0,1:T(8,128)(2,1)S(1)} %fusion.44), channel_id=1, replica_groups=mesh['row'=32,'col'=8] {'row'}, dimensions={0}, use_global_device_ids=true | all-gather | bytes 540672 | tf_op jit(solution)/shard_map/all_gather | solution.py:102
  607.1 0.7 reshape.91
  608.6 0.7 convolution_bitcast_fusion.2
  609.3 0.9 fusion.4
  610.2 0.7 copy.49
  611.0 72.0 %all-reduce.13.cloned.1.call-done = bf16[2,512,64]{1,0,2:T(2,128)(2,1)} async-done(((bf16[2,512,64]{1,0,2:T(2,128)(2,1)}), bf16[2,512,64]{1,0,2:T(2,128)(2,1)}) %all-reduce.13.cloned.1.call-update) | async-done | bytes 131088 | tf_op jit(solution)/shard_map/psum | solution.py:15
  683.0 1.2 convolution_convert_fusion.4
  684.7 1.0 fusion.6
  686.3 77.8 %all-reduce.15.cloned.1.call-done = f32[1024,64]{0,1:T(8,128)} async-done(((f32[1024,64]{0,1:T(8,128)}), f32[1024,64]{0,1:T(8,128)}) %all-reduce.15.cloned.1.call-update) | async-done | bytes 262160 | tf_op jit(solution)/shard_map/psum | solution.py:111
  764.1 1.0 add_dynamic-update-slice_fusion.1
  765.1 1.0 copy-done.3
  766.4 75.2 %psum.106 = f32[32,64]{1,0:T(8,128)S(1)} all-reduce(f32[32,64]{1,0:T(8,128)S(1)} %fusion.20), channel_id=1, replica_groups=mesh['row'=32,'col'=8] {'row','col'}, use_global_device_ids=true, to_apply=%region_17.20 | all-reduce | flops 2048 | bytes 16384 | tf_op jit(solution)/shard_map/psum | solution.py:100
  841.6 43.4 %reduce-scatter.6.cloned.1.call-done = f32[128,64]{0,1:T(8,128)} async-done(((f32[4096,64]{0,1:T(8,128)}), f32[128,64]{0,1:T(8,128)}) %reduce-scatter.6.cloned.1.call-update) | async-done | bytes 32784 | tf_op jit(solution)/shard_map/reduce_scatter | solution.py:113
  885.0 1.1 convolution_add_fusion.1
  886.2 73.2 %psum.107 = f32[64,64]{0,1:T(8,128)S(1)} all-reduce(f32[64,64]{0,1:T(8,128)S(1)} %fusion.76), channel_id=1, replica_groups=mesh['row'=32,'col'=8] {'row','col'}, use_global_device_ids=true, to_apply=%region_18.21 | all-reduce | flops 4096 | bytes 32768 | tf_op jit(solution)/shard_map/psum | solution.py:118
  959.6 5.8 cholesky.70
  965.5 0.6 compare_reduce_fusion.1
  966.1 0.7 fusion.25
  966.8 4.9 custom-call.8
  971.9 39.5 %all_gather.11 = bf16[4096,64]{0,1:T(8,128)(2,1)S(1)} all-gather(bf16[128,64]{0,1:T(8,128)(2,1)S(1)} %fusion.45), channel_id=1, replica_groups=mesh['row'=32,'col'=8] {'row'}, dimensions={0}, use_global_device_ids=true | all-gather | bytes 540672 | tf_op jit(solution)/shard_map/all_gather | solution.py:102
  1011.5 0.7 reshape.95
  1012.8 0.7 convolution_bitcast_fusion
  1013.5 0.9 fusion
  1014.4 0.7 copy.52
  1015.5 72.0 %all-reduce.17.cloned.1.call-done = bf16[2,512,64]{1,0,2:T(2,128)(2,1)} async-done(((bf16[2,512,64]{1,0,2:T(2,128)(2,1)}), bf16[2,512,64]{1,0,2:T(2,128)(2,1)}) %all-reduce.17.cloned.1.call-update) | async-done | bytes 131088 | tf_op jit(solution)/shard_map/psum | solution.py:15
  1087.4 1.2 convolution_convert_fusion.3
  1089.1 1.0 fusion.2
  1090.7 77.9 %all-reduce.19.cloned.1.call-done = f32[1024,64]{0,1:T(8,128)} async-done(((f32[1024,64]{0,1:T(8,128)}), f32[1024,64]{0,1:T(8,128)}) %all-reduce.19.cloned.1.call-update) | async-done | bytes 262160 | tf_op jit(solution)/shard_map/psum | solution.py:111
  1168.7 1.0 add_dynamic-update-slice_fusion
  1169.7 1.0 copy-done.1
  1170.9 75.4 %psum.110 = f32[32,64]{1,0:T(8,128)S(1)} all-reduce(f32[32,64]{1,0:T(8,128)S(1)} %fusion.18), channel_id=1, replica_groups=mesh['row'=32,'col'=8] {'row','col'}, use_global_device_ids=true, to_apply=%region_22.25 | all-reduce | flops 2048 | bytes 16384 | tf_op jit(solution)/shard_map/psum | solution.py:100
  1246.3 43.3 %reduce-scatter.8.cloned.1.call-done = f32[128,64]{0,1:T(8,128)} async-done(((f32[4096,64]{0,1:T(8,128)}), f32[128,64]{0,1:T(8,128)}) %reduce-scatter.8.cloned.1.call-update) | async-done | bytes 32784 | tf_op jit(solution)/shard_map/reduce_scatter | solution.py:113
  1289.6 1.1 convolution_add_fusion
  1290.9 73.3 %psum.111 = f32[64,64]{0,1:T(8,128)S(1)} all-reduce(f32[64,64]{0,1:T(8,128)S(1)} %fusion.77), channel_id=1, replica_groups=mesh['row'=32,'col'=8] {'row','col'}, use_global_device_ids=true, to_apply=%region_23.26 | all-reduce | flops 4096 | bytes 32768 | tf_op jit(solution)/shard_map/psum | solution.py:118
  1364.2 5.8 cholesky.81
  1370.8 0.7 fusion.26
  1371.4 4.9 custom-call.9
  1376.3 0.9 convolution_bitcast_fusion.6
  (81 shorter events, 9.6 us)
Async XLA Ops:
  6.5 153.4 %copy-start.6 = (u32[256]{0:T(256)S(1)}, u32[256]{0:T(256)}, u32[]{:S(2)}) copy-start(u32[256]{0:T(256)} %constant.105) | copy-start | bytes 3076
  6.5 155.4 %copy-start.4 = (f32[1,128,64]{1,2,0:T(8,128)S(1)}, f32[1,128,64]{1,2,0:T(8,128)}, u32[]{:S(2)}) copy-start(f32[1,128,64]{1,2,0:T(8,128)} %param.12) | copy-start | bytes 98308
  6.5 271.8 %all-reduce.9.cloned.1.call-start = ((), (), s32[]{:S(2)}) async-start(), calls=%async_computation.3 | async-start | bytes 262144 | tf_op jit(solution)/shard_map/psum | solution.py:15
  10.8 190.1 %copy-start = (bf16[4,512,512]{2,1,0:T(8,128)(2,1)S(1)}, bf16[4,512,512]{2,1,0:T(8,128)(2,1)}, u32[]{:S(2)}) copy-start(bf16[4,512,512]{2,1,0:T(8,128)(2,1)} %param.8) | copy-start | bytes 6291460
  200.5 159.2 %all-reduce.11.cloned.1.call-start = ((), (), s32[]{:S(2)}) async-start(), calls=%async_computation.4 | async-start | bytes 524288 | tf_op jit(solution)/shard_map/psum | solution.py:111
  203.4 277.1 %reduce-scatter.4.cloned.1.call-start = ((), (), s32[]{:S(2)}) async-start(), calls=%async_computation.5 | async-start | bytes 1081344 | tf_op jit(solution)/shard_map/reduce_scatter | solution.py:113
  281.1 80.6 %copy-start.5 = (s32[32]{0:T(128)S(1)}, s32[32]{0:T(128)}, u32[]{:S(2)}) copy-start(s32[32]{0:T(128)} %param.11) | copy-start | bytes 388
  360.6 1.0 copy-start.2
  361.7 321.3 %all-reduce.13.cloned.1.call-start = ((), (), s32[]{:S(2)}) async-start(), calls=%async_computation.6 | async-start | bytes 262144 | tf_op jit(solution)/shard_map/psum | solution.py:15
  607.9 156.3 %all-reduce.15.cloned.1.call-start = ((), (), s32[]{:S(2)}) async-start(), calls=%async_computation.7 | async-start | bytes 524288 | tf_op jit(solution)/shard_map/psum | solution.py:111
  611.0 274.0 %reduce-scatter.6.cloned.1.call-start = ((), (), s32[]{:S(2)}) async-start(), calls=%async_computation.8 | async-start | bytes 1081344 | tf_op jit(solution)/shard_map/reduce_scatter | solution.py:113
  765.1 1.0 copy-start.3
  766.1 321.3 %all-reduce.17.cloned.1.call-start = ((), (), s32[]{:S(2)}) async-start(), calls=%async_computation.9 | async-start | bytes 262144 | tf_op jit(solution)/shard_map/psum | solution.py:15
  1012.2 156.4 %all-reduce.19.cloned.1.call-start = ((), (), s32[]{:S(2)}) async-start(), calls=%async_computation.10 | async-start | bytes 524288 | tf_op jit(solution)/shard_map/psum | solution.py:111
  1015.2 274.4 %reduce-scatter.8.cloned.1.call-start = ((), (), s32[]{:S(2)}) async-start(), calls=%async_computation.11 | async-start | bytes 1081344 | tf_op jit(solution)/shard_map/reduce_scatter | solution.py:113
  1169.7 1.0 copy-start.1
Sparse Core Ops, SparseCore 0:
  200.6 77.7 all-reduce.8
  281.0 78.5 all-reduce.10
  363.7 116.7 reduce-scatter.3
  608.0 74.9 all-reduce.12
  685.5 78.5 all-reduce.14
  768.0 116.8 reduce-scatter.5
  1012.4 75.0 all-reduce.16
  1090.0 78.5 all-reduce.18
  1172.7 116.8 reduce-scatter.7
where the time goes:
time: 1390 us; the launch traced here: 1380 us
  blocking collectives  712 us (51%)
  waiting for transfers between devices  581 us (42%)
  other arithmetic  44.5 us (3%)
  matrix products  20 us (1%)
  between operations  15 us (1%)
    psum x3, waiting for transfers between devices, shards(): rows_sum = lax.psum(part_rows, 'col')  234 us
    psum x3, blocking collectives, shards(): lax.psum(jnp.dot(member_own.T, basis_own, precision=highest), ('row', 'co...  226 us
    psum x3, blocking collectives, shards(): gram_matrix = lax.psum(gram_part, ('row', 'col'))  220 us
    psum x3, waiting for transfers between devices, broadcast(): return lax.psum(jnp.where(mine, value, jnp.zeros_like(value)), axis)  219 us
    unnamed x1, blocking collectives  132 us
    reduce_scatter x3, waiting for transfers between devices, shards(): lax.psum_scatter(part_cols, 'row', scatter_dimension=0, tiled=True)  129 us
    all_gather x3, blocking collectives, shards(): lax.all_gather((inv_own[:, None] * basis_own).astype(jnp.bfloat16), 'row'...  117 us
  transfers between devices with their start and end apart: 9, of which 9 were waited for; matrix products, arithmetic and copies ran while one was open for 1% of the time, Pallas kernels for 0%

commit v1 on v0

v1 whole, which is shorter than its diff:
```python
import jax
import jax.numpy as jnp
from jax import lax
from jax.sharding import PartitionSpec as P

ROW_BLOCKS = 2
ITERS = 3


highest = lax.Precision.HIGHEST


def membership(first_doc, doc_count, lang_ends, lang_starts):
    doc_index = first_doc + jnp.arange(doc_count, dtype=jnp.int32)
    return (
        (doc_index[:, None] >= lang_starts[None, :]) & (doc_index[:, None] < lang_ends[None, :])
    ).astype(jnp.float32)


def apply_tiles(affinity_tiles, pick_rows, pick_cols, scaled_rows, scaled_cols, col_blocks):
    slot_count, tile_size, _ = affinity_tiles.shape
    vectors = scaled_cols.shape[1]
    blocks_r = scaled_rows.reshape(ROW_BLOCKS, tile_size, vectors)
    blocks_c = scaled_cols.reshape(col_blocks, tile_size, vectors)
    chosen_c = jnp.einsum(
        "tq,qjk->tjk", pick_cols, blocks_c, preferred_element_type=jnp.float32
    ).astype(jnp.bfloat16)
    chosen_r = jnp.einsum(
        "tp,pik->tik", pick_rows, blocks_r, preferred_element_type=jnp.float32
    ).astype(jnp.bfloat16)
    forward = jnp.einsum(
        "tij,tjk->tik", affinity_tiles, chosen_c, preferred_element_type=jnp.float32
    )
    backward = jnp.einsum(
        "tij,tik->tjk", affinity_tiles, chosen_r, preferred_element_type=jnp.float32
    )
    part_rows = jnp.einsum("tp,tik->pik", pick_rows.astype(jnp.float32), forward, precision=highest)
    part_cols = jnp.einsum(
        "tq,tjk->qjk", pick_cols.astype(jnp.float32), backward, precision=highest
    )
    return (
        part_rows.reshape(ROW_BLOCKS * tile_size, vectors),
        part_cols.reshape(col_blocks * tile_size, vectors),
    )


def make_plan(rows, cols):
    group_ratio = rows // cols
    both = ("row", "col")

    def linear(r, c):
        return r * cols + c

    owner_pairs = [
        (linear(r, c), linear((r % group_ratio) * cols + c, r // group_ratio))
        for r in range(rows)
        for c in range(cols)
    ]
    back_pairs = [(dst, src) for src, dst in owner_pairs]

    def to_owner(x):
        return lax.ppermute(x, both, owner_pairs)

    def from_owner(x):
        return lax.ppermute(x, both, back_pairs)

    def halving_scatter(x, axis, size):
        me = lax.axis_index(axis)
        block = x.shape[0] // size
        dist = size // 2
        while dist >= 1:
            upper = (me // dist) % 2
            keep = lax.dynamic_slice_in_dim(x, upper * dist * block, dist * block, 0)
            send = lax.dynamic_slice_in_dim(x, (1 - upper) * dist * block, dist * block, 0)
            pairs = [(i, i ^ dist) for i in range(size)]
            x = keep + lax.ppermute(send, axis, pairs)
            dist //= 2
        return x

    def butterfly_sum(x):
        total = rows * cols
        dist = 1
        while dist < total:
            pairs = [(i, i ^ dist) for i in range(total)]
            x = x + lax.ppermute(x, both, pairs)
            dist *= 2
        return x

    return to_owner, from_owner, halving_scatter, butterfly_sum


def shards(affinity_tiles, tile_rows, tile_cols, lang_counts, start_basis, plan):
    to_owner, from_owner, halving_scatter, butterfly_sum = plan
    row_devices = lax.axis_size("row")
    col_devices = lax.axis_size("col")
    col_blocks = ROW_BLOCKS * row_devices // col_devices
    tile_size = affinity_tiles.shape[1]
    piece_rows = start_basis.shape[1]
    vectors = start_basis.shape[2]
    doc_total = piece_rows * row_devices * col_devices
    my_row = lax.axis_index("row")
    my_col = lax.axis_index("col")
    col_span = col_blocks * tile_size
    piece_offset = my_row * piece_rows
    present = tile_rows >= 0
    local_p = tile_rows - my_row * ROW_BLOCKS
    local_q = tile_cols - my_col * col_blocks
    pick_rows = (
        (local_p[:, None] == jnp.arange(ROW_BLOCKS, dtype=jnp.int32)[None, :]) & present[:, None]
    ).astype(jnp.bfloat16)
    pick_cols = (
        (local_q[:, None] == jnp.arange(col_blocks, dtype=jnp.int32)[None, :]) & present[:, None]
    ).astype(jnp.bfloat16)

    def to_own(rows_part, cols_part):
        from_cols = lax.psum_scatter(cols_part, "row", scatter_dimension=0, tiled=True)
        from_rows = to_owner(halving_scatter(rows_part, "col", col_devices))
        return from_cols + from_rows

    def gather_groups(own):
        cols_all = lax.all_gather(own, "row", axis=0, tiled=True)
        rows_all = lax.all_gather(from_owner(own), "col", axis=0, tiled=True)
        return cols_all, rows_all

    magnitude = jnp.abs(affinity_tiles)
    row_mass = jnp.sum(magnitude, axis=2, dtype=jnp.float32)
    col_mass = jnp.sum(magnitude, axis=1, dtype=jnp.float32)
    degree_rows = jnp.einsum(
        "tp,ti->pi", pick_rows.astype(jnp.float32), row_mass, precision=highest
    ).reshape(ROW_BLOCKS * tile_size, 1)
    degree_cols = jnp.einsum(
        "tq,tj->qj", pick_cols.astype(jnp.float32), col_mass, precision=highest
    ).reshape(col_span, 1)
    inv_own = lax.rsqrt(1.0 + to_own(degree_rows, degree_cols))
    lang_ends = jnp.cumsum(lang_counts)
    lang_starts = lang_ends - lang_counts
    counts_real = lang_counts.astype(jnp.float32)
    member_own = membership(my_col * col_span + piece_offset, piece_rows, lang_ends, lang_starts)
    basis_own = start_basis[0]
    langs = member_own.shape[1]
    first = jnp.concatenate(
        [
            jnp.dot(member_own.T, basis_own, precision=highest),
            jnp.broadcast_to(jnp.sum(inv_own), (1, vectors)),
        ],
        axis=0,
    )
    packed = jnp.concatenate([basis_own, inv_own], axis=1)
    cols_all, rows_all = gather_groups(packed)
    first = butterfly_sum(first)
    lang_now = first[:langs]
    prior_scale = first[langs, 0] / doc_total
    basis_cols, inv_cols = cols_all[:, :vectors], cols_all[:, vectors:]
    basis_rows, inv_rows = rows_all[:, :vectors], rows_all[:, vectors:]
    for iteration in range(ITERS):
        last = iteration == ITERS - 1
        lang_mean = prior_scale * (lang_now / counts_real[:, None])
        scaled_cols = (inv_cols * basis_cols).astype(jnp.bfloat16)
        scaled_rows = (inv_rows * basis_rows).astype(jnp.bfloat16)
        part_rows, part_cols = apply_tiles(
            affinity_tiles, pick_rows, pick_cols, scaled_rows, scaled_cols, col_blocks
        )
        product_own = to_own(part_rows, part_cols)
        applied_own = inv_own * product_own + jnp.dot(member_own, lang_mean, precision=highest)
        gram_part = jnp.dot(applied_own.T, applied_own, precision=highest)
        if last:
            gram_matrix = butterfly_sum(gram_part)
        else:
            lang_part = jnp.dot(member_own.T, applied_own, precision=highest)
            sums = butterfly_sum(jnp.concatenate([gram_part, lang_part], axis=0))
            gram_matrix = sums[:vectors]
            applied_cols, applied_rows = gather_groups(applied_own)
        factor = jnp.linalg.cholesky(gram_matrix / doc_total)
        factor_inv = jax.scipy.linalg.solve_triangular(
            factor, jnp.eye(vectors, dtype=jnp.float32), lower=True
        )
        if last:
            basis_own = jnp.dot(applied_own, factor_inv.T, precision=highest)
        else:
            lang_now = jnp.dot(sums[vectors:], factor_inv.T, precision=highest)
            basis_cols = jnp.dot(applied_cols, factor_inv.T, precision=highest)
            basis_rows = jnp.dot(applied_rows, factor_inv.T, precision=highest)
    return basis_own[None]


def solution(mesh):
    plan = make_plan(mesh.shape["row"], mesh.shape["col"])
    in_specs = (
        P(("row", "col"), None, None),
        P(("row", "col")),
        P(("row", "col")),
        P(),
        P("col", "row", None),
    )
    out_specs = P("col", "row", None)

    def body(*args):
        return shards(*args, plan)

    return jax.shard_map(body, mesh=mesh, in_specs=in_specs, out_specs=out_specs, check_vma=False)
```

time: 1390 us -> 840 us (0.60)
  blocking collectives: 712 us -> 82 us
  starting transfers between devices: 0.74 us -> 90.1 us
  waiting for transfers between devices: 581 us -> 565 us
    psum x7 -> x0, blocking collectives: 462 us -> none  [the longest x3 226 us: shards(): lax.psum(jnp.dot(member_own.T, basis_own, precision=highest), ('row', 'co...]
    psum x6 -> x0, waiting for transfers between devices: 452 us -> none  [the longest x3 234 us: shards(): rows_sum = lax.psum(part_rows, 'col')]
    unnamed x1 -> x0, blocking collectives: 132 us -> none
    ppermute x0 -> x51, waiting for transfers between devices: none -> 127 us  [the longest x32 82.4 us: butterfly_sum(): x = x + lax.ppermute(x, both, pairs)]
    reduce_scatter x3, waiting for transfers between devices: 129 us -> 250 us  [to_own(): lax.psum_scatter(cols_part, 'row', scatter_dimension=0, tiled=True)]
    unnamed x9 -> x8, waiting for transfers between devices: 0.15 us -> 116 us
    ppermute x0 -> x51, starting transfers between devices: none -> 89.6 us  [the longest x32 42.5 us: butterfly_sum(): x = x + lax.ppermute(x, both, pairs)]
    all_gather x0 -> x3, waiting for transfers between devices: none -> 72.2 us  [gather_groups(): cols_all = lax.all_gather(own, 'row', axis=0, tiled=True)]
  transfers between devices with their start and end apart: 9 -> 58, of which waited for: 9 -> 45; matrix products, arithmetic and copies ran while one was open for 1% -> 7% of each run, Pallas kernels for 0% -> 0%
where the time goes in v1:
time: 840 us; the launch traced here: 831 us
  waiting for transfers between devices  565 us (67%)
  starting transfers between devices  90.1 us (11%)
  blocking collectives  82 us (10%)
  other arithmetic  45.6 us (5%)
  matrix products  21.7 us (3%)
  between operations  15.4 us (2%)
  local copies, waits for them, and re-layouts  11.1 us (1%)
    reduce_scatter x3, waiting for transfers between devices, to_own(): lax.psum_scatter(cols_part, 'row', scatter_dimension=0, tiled=True)  250 us
    unnamed x8, waiting for transfers between devices  116 us
    ppermute x32, waiting for transfers between devices, butterfly_sum(): x = x + lax.ppermute(x, both, pairs)  82.4 us
    all_gather x3, blocking collectives, gather_groups(): rows_all = lax.all_gather(from_owner(own), 'col', axis=0, tiled=True)  82 us
    all_gather x3, waiting for transfers between devices, gather_groups(): cols_all = lax.all_gather(own, 'row', axis=0, tiled=True)  72.2 us
    ppermute x32, starting transfers between devices, butterfly_sum(): x = x + lax.ppermute(x, both, pairs)  42.5 us
    ppermute x12, waiting for transfers between devices, halving_scatter(): x = keep + lax.ppermute(send, axis, pairs)  38.1 us
    ppermute x4, starting transfers between devices, to_owner(): return lax.ppermute(x, both, owner_pairs)  20.7 us
  transfers between devices with their start and end apart: 58, of which 45 were waited for; matrix products, arithmetic and copies ran while one was open for 7% of the time, Pallas kernels for 0%

profile of v1, /device:TPU:6, one launch (start us, length us, event | category | flops | bytes accessed | tf_op | source)
XLA Modules:
  0.0 831.3 jit_solution(17117660706377148428)
XLA Ops:
  7.9 2.2 convert_reduce_fusion
  11.8 3.7 collective-permute-done
  16.4 2.7 collective-permute-done.1
  23.0 6.2 collective-permute-start.3
  29.2 116.3 %reduce-scatter.13.cloned.1.call-done = f32[128,1]{1,0:T(8,128)} async-done(((f32[4096,1]{1,0:T(8,128)}), f32[128,1]{1,0:T(8,128)}) %reduce-scatter.13.cloned.1.call-update) | async-done | bytes 528
  147.7 4.0 collective-permute-start.4
  152.0 6.3 collective-permute-done.4
  158.2 26.5 %all_gather.18 = f32[1024,65]{0,1:T(8,128)S(1)} all-gather(f32[128,65]{0,1:T(8,128)S(1)} %collective-permute-done.4), channel_id=1, replica_groups=mesh['row'=32,'col'=8] {'col'}, dimensions={0}, use_global_device_ids=true | all-gather | bytes 299520 | tf_op jit(solution)/shard_map/all_gather | solution.py:122
  188.4 30.1 %all-gather.4.cloned.1.call-done = f32[4096,65]{0,1:T(8,128)} async-done(((f32[128,65]{0,1:T(8,128)}), f32[4096,65]{0,1:T(8,128)}) %all-gather.4.cloned.1.call-update) | async-done | bytes 1064976 | tf_op jit(solution)/shard_map/all_gather | solution.py:121
  224.4 5.7 collective-permute-done.5
  237.8 2.7 collective-permute-done.10
  241.8 4.1 collective-permute-done.11
  248.8 5.5 collective-permute-start.8
  254.7 3.6 collective-permute-done.14
  259.8 3.4 collective-permute-done.15
  263.1 4.2 collective-permute-start.16
  267.3 3.5 collective-permute-done.16
  272.0 64.2 %reduce-scatter.7.cloned.1.call-done = f32[128,64]{0,1:T(8,128)} async-done(((f32[4096,64]{0,1:T(8,128)}), f32[128,64]{0,1:T(8,128)}) %reduce-scatter.7.cloned.1.call-update) | async-done | bytes 32784 | tf_op jit(solution)/shard_map/reduce_scatter | solution.py:116
  338.4 3.3 collective-permute-done.18
  342.7 3.1 collective-permute-done.19
  347.2 4.0 collective-permute-done.20
  354.2 3.6 collective-permute-done.22
  358.4 4.6 collective-permute-start.17
  363.9 4.0 collective-permute-done.24
  367.9 3.5 collective-permute-start.25
  371.4 27.6 %all_gather.20 = f32[1024,64]{0,1:T(8,128)S(1)} all-gather(f32[128,64]{0,1:T(8,128)S(1)} %collective-permute-done.17), channel_id=1, replica_groups=mesh['row'=32,'col'=8] {'col'}, dimensions={0}, use_global_device_ids=true | all-gather | bytes 294912 | tf_op jit(solution)/shard_map/all_gather | solution.py:122
  399.1 5.8 cholesky.59
  406.5 4.9 custom-call.7
  415.7 21.1 %all-gather.6.cloned.1.call-done = f32[4096,64]{0,1:T(8,128)} async-done(((f32[128,64]{0,1:T(8,128)}), f32[4096,64]{0,1:T(8,128)}) %all-gather.6.cloned.1.call-update) | async-done | bytes 1048592 | tf_op jit(solution)/shard_map/all_gather | solution.py:121
  436.8 2.3 fusion
  442.8 5.7 collective-permute-done.26
  449.5 3.4 collective-permute-done.27
  453.9 3.1 collective-permute-done.28
  457.0 4.5 collective-permute-start.29
  461.8 92.8 %reduce-scatter.9.cloned.1.call-done = f32[128,64]{0,1:T(8,128)} async-done(((f32[4096,64]{0,1:T(8,128)}), f32[128,64]{0,1:T(8,128)}) %reduce-scatter.9.cloned.1.call-update) | async-done | bytes 32784 | tf_op jit(solution)/shard_map/reduce_scatter | solution.py:116
  556.5 3.4 collective-permute-done.31
  560.8 3.1 collective-permute-done.32
  565.3 4.0 collective-permute-done.33
  572.3 3.6 collective-permute-done.35
  576.6 4.6 collective-permute-start.30
  582.1 3.9 collective-permute-done.37
  586.1 3.5 collective-permute-start.38
  589.5 27.8 %all_gather.22 = f32[1024,64]{0,1:T(8,128)S(1)} all-gather(f32[128,64]{0,1:T(8,128)S(1)} %collective-permute-done.30), channel_id=1, replica_groups=mesh['row'=32,'col'=8] {'col'}, dimensions={0}, use_global_device_ids=true | all-gather | bytes 294912 | tf_op jit(solution)/shard_map/all_gather | solution.py:122
  617.4 5.8 cholesky.70
  624.7 4.9 custom-call.8
  633.7 20.9 %all-gather.8.cloned.1.call-done = f32[4096,64]{0,1:T(8,128)} async-done(((f32[128,64]{0,1:T(8,128)}), f32[4096,64]{0,1:T(8,128)}) %all-gather.8.cloned.1.call-update) | async-done | bytes 1048592 | tf_op jit(solution)/shard_map/all_gather | solution.py:121
  654.7 2.3 fusion.1
  660.7 5.7 collective-permute-done.39
  667.4 3.4 collective-permute-done.40
  671.8 3.1 collective-permute-done.41
  674.8 4.5 collective-permute-start.42
  679.6 93.0 %reduce-scatter.11.cloned.1.call-done = f32[128,64]{0,1:T(8,128)} async-done(((f32[4096,64]{0,1:T(8,128)}), f32[128,64]{0,1:T(8,128)}) %reduce-scatter.11.cloned.1.call-update) | async-done | bytes 32784 | tf_op jit(solution)/shard_map/reduce_scatter | solution.py:116
  774.2 3.3 collective-permute-done.43
  778.4 3.1 collective-permute-done.44
  783.0 3.9 collective-permute-done.45
  788.1 2.3 collective-permute-start.47
  790.4 3.5 collective-permute-done.47
  794.5 3.3 collective-permute-done.48
  797.8 2.4 collective-permute-start.49
  800.1 2.8 collective-permute-done.49
  802.9 4.0 collective-permute-start.50
  806.9 3.9 collective-permute-done.50
  810.9 5.8 cholesky.81
  818.0 4.9 custom-call.9
  (231 shorter events, 83.5 us)
Async XLA Ops:
  6.5 5.2 copy-start.5
  6.5 138.9 %reduce-scatter.13.cloned.1.call-start = ((), (), s32[]{:S(2)}) async-start(), calls=%async_computation.10 | async-start | bytes 2162688
  10.3 5.2 collective-permute-start
  15.5 3.6 collective-permute-start.1
  19.0 3.9 collective-permute-start.2
  20.8 126.1 %copy-start.3 = (f32[1,128,64]{1,2,0:T(8,128)S(1)}, f32[1,128,64]{1,2,0:T(8,128)}, u32[]{:S(2)}) copy-start(f32[1,128,64]{1,2,0:T(8,128)} %param.12) | copy-start | bytes 98308
  20.8 130.8 %copy-start.4 = (s32[32]{0:T(128)S(1)}, s32[32]{0:T(128)}, u32[]{:S(2)}) copy-start(s32[32]{0:T(128)} %param.11) | copy-start | bytes 388
  22.9 162.4 %copy-start = (bf16[4,512,512]{2,1,0:T(8,128)(2,1)S(1)}, bf16[4,512,512]{2,1,0:T(8,128)(2,1)}, u32[]{:S(2)}) copy-start(bf16[4,512,512]{2,1,0:T(8,128)(2,1)} %param.8) | copy-start | bytes 6291460
  22.9 195.6 %all-gather.4.cloned.1.call-start = ((), (), s32[]{:S(2)}) async-start(), calls=%async_computation.5 | async-start | bytes 1216512 | tf_op jit(solution)/shard_map/all_gather | solution.py:121
  23.0 123.4 %collective-permute-start.3 = (f32[128,1]{0,1:T(1,128)S(1)}, f32[128,1]{0,1:T(1,128)S(1)}, u32[]{:S(2)}, u32[]{:S(2)}) collective-permute-start(f32[128,1]{0,1:T(1,128)S(1)} %fusion.67), channel_id=1, source_target_pairs={{0,0},{1,8},{2,16},{3,24},{4,32},{5,40},{6,48},{7,56},{8,64},{9,72... | collective-permute-start | bytes 1544 | tf_op jit(solution)/shard_map/ppermute | solution.py:62
  147.6 188.5 %reduce-scatter.7.cloned.1.call-start = ((), (), s32[]{:S(2)}) async-start(), calls=%async_computation.4 | async-start | bytes 1081344 | tf_op jit(solution)/shard_map/reduce_scatter | solution.py:116
  147.7 10.6 %collective-permute-start.4 = (f32[128,65]{0,1:T(8,128)}, f32[128,65]{0,1:T(8,128)S(1)}, u32[]{:S(2)}, u32[]{:S(2)}) collective-permute-start(f32[128,65]{0,1:T(8,128)} %pad_maximum_fusion), channel_id=1, source_target_pairs={{0,0},{8,1},{16,2},{24,3},{32,4},{40,5},{48,6},{56,7},{64,8},{72,9... | collective-permute-start | bytes 99848 | tf_op jit(solution)/shard_map/ppermute | solution.py:65
  188.3 248.5 %all-gather.6.cloned.1.call-start = ((), (), s32[]{:S(2)}) async-start(), calls=%async_computation.7 | async-start | bytes 1081344 | tf_op jit(solution)/shard_map/all_gather | solution.py:121
  222.9 7.2 collective-permute-start.5
  230.2 4.4 collective-permute-start.6
  232.1 4.0 collective-permute-start.9
  234.6 14.2 %collective-permute-start.7 = (f32[128,64]{0,1:T(8,128)S(1)}, f32[128,64]{0,1:T(8,128)S(1)}, u32[]{:S(2)}, u32[]{:S(2)}) collective-permute-start(f32[128,64]{0,1:T(8,128)S(1)} %constant_dynamic-slice_fusion.6), channel_id=1, source_target_pairs={{0,1},{1,0},{2,3},{3,2},{4,5},{5,4},{6,7},{7,6},{8,9},{9,8},{10,11... | collective-permute-start | bytes 98312 | tf_op jit(solution)/shard_map/ppermute | solution.py:76
  236.7 3.9 collective-permute-start.10
  240.6 5.3 collective-permute-start.11
  245.9 1.6 collective-permute-start.12
  247.5 6.7 collective-permute-start.13
  248.8 87.4 %collective-permute-start.8 = (f32[128,64]{0,1:T(8,128)S(1)}, f32[128,64]{0,1:T(8,128)S(1)}, u32[]{:S(2)}, u32[]{:S(2)}) collective-permute-start(f32[128,64]{0,1:T(8,128)S(1)} %dynamic-slice_add_fusion.8), channel_id=1, source_target_pairs={{0,0},{1,8},{2,16},{3,24},{4,32},{5,40},{6,48},{7,56},{8,64},{9,72... | collective-permute-start | bytes 98312 | tf_op jit(solution)/shard_map/ppermute | solution.py:62
  254.3 4.0 collective-permute-start.14
  258.3 4.8 collective-permute-start.15
  263.1 7.7 collective-permute-start.16
  337.2 26.6 %copy-start.2 = (f32[128,64]{0,1:T(8,128)}, f32[128,64]{0,1:T(8,128)S(1)}, u32[]{:S(2)}) copy-start(f32[128,64]{0,1:T(8,128)S(1)} %multiply_add_fusion.2) | copy-start | bytes 98308
  337.8 3.9 collective-permute-start.18
  341.8 3.9 collective-permute-start.19
  345.7 5.4 collective-permute-start.20
  351.1 1.2 collective-permute-start.21
  352.4 5.4 collective-permute-start.22
  357.8 5.2 collective-permute-start.23
  358.4 13.0 %collective-permute-start.17 = (f32[128,64]{0,1:T(8,128)S(1)}, f32[128,64]{0,1:T(8,128)S(1)}, u32[]{:S(2)}, u32[]{:S(2)}) collective-permute-start(f32[128,64]{0,1:T(8,128)S(1)} %multiply_add_fusion.2), channel_id=1, source_target_pairs={{0,0},{8,1},{16,2},{24,3},{32,4},{40,5},{48,6},{56,7},{64,8},{72,9... | collective-permute-start | bytes 98312 | tf_op jit(solution)/shard_map/ppermute | solution.py:65
  363.0 4.9 collective-permute-start.24
  363.9 190.7 %reduce-scatter.9.cloned.1.call-start = ((), (), s32[]{:S(2)}) async-start(), calls=%async_computation.6 | async-start | bytes 1081344 | tf_op jit(solution)/shard_map/reduce_scatter | solution.py:116
  367.9 31.1 %collective-permute-start.25 = (f32[96,64]{0,1:T(8,128)S(1)}, f32[96,64]{0,1:T(8,128)S(1)}, u32[]{:S(2)}, u32[]{:S(2)}) collective-permute-start(f32[96,64]{0,1:T(8,128)S(1)} %add.286), channel_id=1, source_target_pairs={{0,128},{1,129},{2,130},{3,131},{4,132},{5,133},{6,134},{7,135},{8... | collective-permute-start | bytes 73736 | tf_op jit(solution)/shard_map/ppermute | solution.py:85
  415.4 239.2 %all-gather.8.cloned.1.call-start = ((), (), s32[]{:S(2)}) async-start(), calls=%async_computation.9 | async-start | bytes 1081344 | tf_op jit(solution)/shard_map/all_gather | solution.py:121
  441.3 7.2 collective-permute-start.26
  448.6 4.4 collective-permute-start.27
  452.9 4.0 collective-permute-start.28
  457.0 97.6 %collective-permute-start.29 = (f32[128,64]{0,1:T(8,128)S(1)}, f32[128,64]{0,1:T(8,128)S(1)}, u32[]{:S(2)}, u32[]{:S(2)}) collective-permute-start(f32[128,64]{0,1:T(8,128)S(1)} %dynamic-slice_add_fusion.7), channel_id=1, source_target_pairs={{0,0},{1,8},{2,16},{3,24},{4,32},{5,40},{6,48},{7,56},{8,64},{9,72... | collective-permute-start | bytes 98312 | tf_op jit(solution)/shard_map/ppermute | solution.py:62
  555.4 26.7 %copy-start.1 = (f32[128,64]{0,1:T(8,128)}, f32[128,64]{0,1:T(8,128)S(1)}, u32[]{:S(2)}) copy-start(f32[128,64]{0,1:T(8,128)S(1)} %multiply_add_fusion.1) | copy-start | bytes 98308
  555.9 3.9 collective-permute-start.31
  559.9 3.9 collective-permute-start.32
  563.9 5.4 collective-permute-start.33
  569.3 1.2 collective-permute-start.34
  570.5 5.4 collective-permute-start.35
  575.9 5.2 collective-permute-start.36
  576.6 13.0 %collective-permute-start.30 = (f32[128,64]{0,1:T(8,128)S(1)}, f32[128,64]{0,1:T(8,128)S(1)}, u32[]{:S(2)}, u32[]{:S(2)}) collective-permute-start(f32[128,64]{0,1:T(8,128)S(1)} %multiply_add_fusion.1), channel_id=1, source_target_pairs={{0,0},{8,1},{16,2},{24,3},{32,4},{40,5},{48,6},{56,7},{64,8},{72,9... | collective-permute-start | bytes 98312 | tf_op jit(solution)/shard_map/ppermute | solution.py:65
  581.1 4.9 collective-permute-start.37
  582.1 190.5 %reduce-scatter.11.cloned.1.call-start = ((), (), s32[]{:S(2)}) async-start(), calls=%async_computation.8 | async-start | bytes 1081344 | tf_op jit(solution)/shard_map/reduce_scatter | solution.py:116
  586.1 31.2 %collective-permute-start.38 = (f32[96,64]{0,1:T(8,128)S(1)}, f32[96,64]{0,1:T(8,128)S(1)}, u32[]{:S(2)}, u32[]{:S(2)}) collective-permute-start(f32[96,64]{0,1:T(8,128)S(1)} %add.299), channel_id=1, source_target_pairs={{0,128},{1,129},{2,130},{3,131},{4,132},{5,133},{6,134},{7,135},{8... | collective-permute-start | bytes 73736 | tf_op jit(solution)/shard_map/ppermute | solution.py:85
  659.2 7.2 collective-permute-start.39
  666.4 4.4 collective-permute-start.40
  670.8 4.0 collective-permute-start.41
  674.8 97.7 %collective-permute-start.42 = (f32[128,64]{0,1:T(8,128)S(1)}, f32[128,64]{0,1:T(8,128)S(1)}, u32[]{:S(2)}, u32[]{:S(2)}) collective-permute-start(f32[128,64]{0,1:T(8,128)S(1)} %dynamic-slice_add_fusion.6), channel_id=1, source_target_pairs={{0,0},{1,8},{2,16},{3,24},{4,32},{5,40},{6,48},{7,56},{8,64},{9,72... | collective-permute-start | bytes 98312 | tf_op jit(solution)/shard_map/ppermute | solution.py:62
  773.5 4.0 collective-permute-start.43
  777.5 3.9 collective-permute-start.44
  781.5 5.4 collective-permute-start.45
  786.9 1.2 collective-permute-start.46
  788.1 5.7 collective-permute-start.47
  793.8 3.9 collective-permute-start.48
  797.8 5.2 collective-permute-start.49
  802.9 7.8 collective-permute-start.50
Sparse Core Ops, SparseCore 0:
  23.0 122.3 reduce-scatter.12
  148.0 70.4 all-gather.3
  222.6 113.5 reduce-scatter.6
  364.0 72.7 all-gather.5
  440.7 113.8 reduce-scatter.8
  582.2 72.4 all-gather.7
  658.7 113.7 reduce-scatter.10

commit v2 on v1

--- a/solution.py
+++ b/solution.py
@@ -66,16 +66,33 @@
 
     def halving_scatter(x, axis, size):
         me = lax.axis_index(axis)
+        bits = size.bit_length() - 1
         block = x.shape[0] // size
-        dist = size // 2
-        while dist >= 1:
-            upper = (me // dist) % 2
-            keep = lax.dynamic_slice_in_dim(x, upper * dist * block, dist * block, 0)
-            send = lax.dynamic_slice_in_dim(x, (1 - upper) * dist * block, dist * block, 0)
-            pairs = [(i, i ^ dist) for i in range(size)]
+        rest = x.shape[1:]
+        x = x.reshape((2,) * bits + (block,) + rest)
+        for bit in range(bits):
+            place = bits - 1 - bit
+            mine = (me >> bit) & 1
+            keep = lax.dynamic_index_in_dim(x, mine, axis=place, keepdims=False)
+            send = lax.dynamic_index_in_dim(x, 1 - mine, axis=place, keepdims=False)
+            pairs = [(i, i ^ (1 << bit)) for i in range(size)]
             x = keep + lax.ppermute(send, axis, pairs)
-            dist //= 2
-        return x
+        return x.reshape((block,) + rest)
+
+    def doubling_gather(x, axis, size):
+        me = lax.axis_index(axis)
+        bits = size.bit_length() - 1
+        block = x.shape[0]
+        rest = x.shape[1:]
+        for step in range(bits):
+            bit = bits - 1 - step
+            upper = ((me >> bit) & 1) == 1
+            pairs = [(i, i ^ (1 << bit)) for i in range(size)]
+            other = lax.ppermute(x, axis, pairs)
+            low = jnp.where(upper, other, x)
+            high = jnp.where(upper, x, other)
+            x = jnp.stack([low, high], axis=step)
+        return x.reshape((size * block,) + rest)
 
     def butterfly_sum(x):
         total = rows * cols
@@ -86,11 +103,11 @@
             dist *= 2
         return x
 
-    return to_owner, from_owner, halving_scatter, butterfly_sum
+    return to_owner, from_owner, halving_scatter, doubling_gather, butterfly_sum
 
 
 def shards(affinity_tiles, tile_rows, tile_cols, lang_counts, start_basis, plan):
-    to_owner, from_owner, halving_scatter, butterfly_sum = plan
+    to_owner, from_owner, halving_scatter, doubling_gather, butterfly_sum = plan
     row_devices = lax.axis_size("row")
     col_devices = lax.axis_size("col")
     col_blocks = ROW_BLOCKS * row_devices // col_devices
@@ -113,13 +130,13 @@
     ).astype(jnp.bfloat16)
 
     def to_own(rows_part, cols_part):
-        from_cols = lax.psum_scatter(cols_part, "row", scatter_dimension=0, tiled=True)
+        from_cols = halving_scatter(cols_part, "row", row_devices)
         from_rows = to_owner(halving_scatter(rows_part, "col", col_devices))
         return from_cols + from_rows
 
     def gather_groups(own):
-        cols_all = lax.all_gather(own, "row", axis=0, tiled=True)
-        rows_all = lax.all_gather(from_owner(own), "col", axis=0, tiled=True)
+        cols_all = doubling_gather(own, "row", row_devices)
+        rows_all = doubling_gather(from_owner(own), "col", col_devices)
         return cols_all, rows_all
 
     magnitude = jnp.abs(affinity_tiles)

time: 840 us -> 420 us (0.50)
  waiting for transfers between devices: 565 us -> 133 us
  blocking collectives: 82 us -> 0 us
  starting transfers between devices: 90.1 us -> 168 us
  local copies, waits for them, and re-layouts: 11.1 us -> 34.6 us
  between operations: 15.4 us -> 2.83 us
  other arithmetic: 45.6 us -> 54.8 us
    reduce_scatter x3 -> x0, waiting for transfers between devices: 250 us -> none  [to_own(): lax.psum_scatter(cols_part, 'row', scatter_dimension=0, tiled=True)]
    unnamed x8 -> x0, waiting for transfers between devices: 116 us -> none
    all_gather x3 -> x0, blocking collectives: 82 us -> none  [gather_groups(): rows_all = lax.all_gather(from_owner(own), 'col', axis=0, tiled=True)]
    all_gather x3 -> x0, waiting for transfers between devices: 72.2 us -> none  [gather_groups(): cols_all = lax.all_gather(own, 'row', axis=0, tiled=True)]
    ppermute x12 -> x32, starting transfers between devices: 13.4 us -> 51.6 us  [halving_scatter(): x = keep + lax.ppermute(send, axis, pairs)]
    ppermute x0 -> x24, starting transfers between devices: none -> 36.4 us  [doubling_gather(): other = lax.ppermute(x, axis, pairs)]
    ppermute x3, waiting for transfers between devices: 6.29 us -> 20 us  [from_owner(): return lax.ppermute(x, both, back_pairs)]
    another operation x1 -> x18, local copies, waits for them, and re-layouts: 0.09 us -> 12.8 us  [the longest x9 6.9 us: doubling_gather(): x = jnp.stack([low, high], axis=step)]
  transfers between devices with their start and end apart: 58 -> 95, of which waited for: 45 -> 54; matrix products, arithmetic and copies ran while one was open for 7% -> 21% of each run, Pallas kernels for 0% -> 0%
where the time goes in v2:
time: 420 us; the launch traced here: 412 us
  starting transfers between devices  168 us (40%)
  waiting for transfers between devices  133 us (32%)
  other arithmetic  54.8 us (13%)
  local copies, waits for them, and re-layouts  34.6 us (8%)
  matrix products  18.5 us (4%)
    ppermute x32, waiting for transfers between devices, butterfly_sum(): x = x + lax.ppermute(x, both, pairs)  72.3 us
    ppermute x32, starting transfers between devices, halving_scatter(): x = keep + lax.ppermute(send, axis, pairs)  51.6 us
    ppermute x32, starting transfers between devices, butterfly_sum(): x = x + lax.ppermute(x, both, pairs)  47.6 us
    ppermute x24, starting transfers between devices, doubling_gather(): other = lax.ppermute(x, axis, pairs)  36.4 us
    ppermute x32, waiting for transfers between devices, halving_scatter(): x = keep + lax.ppermute(send, axis, pairs)  30.6 us
    ppermute x4, starting transfers between devices, to_owner(): return lax.ppermute(x, both, owner_pairs)  23.9 us
    ppermute x3, waiting for transfers between devices, from_owner(): return lax.ppermute(x, both, back_pairs)  20 us
    another operation x9, other arithmetic, shards(): factor = jnp.linalg.cholesky(gram_matrix / doc_total)  19.6 us
  transfers between devices with their start and end apart: 95, of which 54 were waited for; matrix products, arithmetic and copies ran while one was open for 21% of the time, Pallas kernels for 0%

profile of v2, /device:TPU:6, one launch (start us, length us, event | category | flops | bytes accessed | tf_op | source)
XLA Modules:
  0.0 411.6 jit_solution(8378229716705958231)
XLA Ops:
  0.7 2.2 convert_reduce_fusion.1
  6.8 3.3 collective-permute-start.1
  10.9 2.7 collective-permute-done.6
  17.3 3.4 collective-permute-start.3
  20.7 4.6 %collective-permute-start.8 = (f32[128,1]{0,1:T(1,128)S(1)}, f32[128,1]{0,1:T(1,128)S(1)}, u32[]{:S(2)}, u32[]{:S(2)}) collective-permute-start(f32[128,1]{0,1:T(1,128)S(1)} %fusion.91), channel_id=1, source_target_pairs={{0,0},{1,8},{2,16},{3,24},{4,32},{5,40},{6,48},{7,56},{8,64},{9,72... | collective-permute-start | bytes 1544 | tf_op jit(solution)/shard_map/ppermute | solution.py:62
  25.4 4.9 %collective-permute-start.4 = (f32[128,1]{0,1:T(1,128)S(1)}, f32[128,1]{0,1:T(1,128)S(1)}, u32[]{:S(2)}, u32[]{:S(2)}) collective-permute-start(f32[128,1]{0,1:T(1,128)S(1)} %fusion.89), channel_id=1, source_target_pairs={{0,128},{8,136},{16,144},{24,152},{32,160},{40,168},{48,176},{56,1... | collective-permute-start | bytes 1544 | tf_op jit(solution)/shard_map/ppermute | solution.py:79
  30.6 2.4 collective-permute-done.4
  33.6 4.9 %collective-permute-start.18 = (f32[128,65]{0,1:T(8,128)S(1)}, f32[128,65]{0,1:T(8,128)S(1)}, u32[]{:S(2)}, u32[]{:S(2)}) collective-permute-start(f32[128,65]{0,1:T(8,128)S(1)} %pad_maximum_fusion.24), channel_id=1, source_target_pairs={{0,128},{8,136},{16,144},{24,152},{32,160},{40,168},{48,176},{56,1... | collective-permute-start | bytes 99848 | tf_op jit(solution)/shard_map/ppermute | solution.py:91
  43.0 6.3 %collective-permute-done.9 = f32[128,65]{0,1:T(8,128)S(1)} collective-permute-done((f32[128,65]{0,1:T(8,128)S(1)}, f32[128,65]{0,1:T(8,128)S(1)}, u32[]{:S(2)}, u32[]{:S(2)}) %collective-permute-start.9) | collective-permute-done | bytes 33312 | tf_op jit(solution)/shard_map/ppermute | solution.py:65
  49.4 2.6 collective-permute-start.19
  52.0 2.8 collective-permute-done.10
  56.6 2.6 collective-permute-done.11
  62.1 6.0 %collective-permute-start.21 = (f32[2,2,2,128,65]{3,0,4,1,2:T(2,128)}, f32[2,2,2,128,65]{3,0,4,1,2:T(2,128)}, u32[]{:S(2)}, u32[]{:S(2)}) collective-permute-start(f32[2,2,2,128,65]{3,0,4,1,2:T(2,128)} %pad_maximum_fusion.7), channel_id=1, source_target_pairs={{0,16},{8,24},{16,0},{24,8},{32,48},{40,56},{48,32},{56,40},{64,80... | collective-permute-start | bytes 798728 | tf_op jit(solution)/shard_map/ppermute | solution.py:91
  72.1 2.6 constant_dynamic-slice_fusion.13
  80.2 3.0 collective-permute-done.28
  92.1 2.2 reshape.128
  112.2 6.6 %collective-permute-start.26 = (f32[128,64]{0,1:T(8,128)S(1)}, f32[128,64]{0,1:T(8,128)S(1)}, u32[]{:S(2)}, u32[]{:S(2)}) collective-permute-start(f32[128,64]{0,1:T(8,128)S(1)} %bitcast_add_fusion.22), channel_id=1, source_target_pairs={{0,0},{1,8},{2,16},{3,24},{4,32},{5,40},{6,48},{7,56},{8,64},{9,72... | collective-permute-start | bytes 98312 | tf_op jit(solution)/shard_map/ppermute | solution.py:62
  120.3 2.4 collective-permute-done.32
  124.1 3.3 collective-permute-done.33
  127.4 3.9 collective-permute-start.34
  131.3 3.8 collective-permute-done.34
  137.4 4.0 collective-permute-start.52
  145.3 6.6 %collective-permute-done.35 = f32[128,64]{0,1:T(8,128)S(1)} collective-permute-done((f32[128,64]{0,1:T(8,128)S(1)}, f32[128,64]{0,1:T(8,128)S(1)}, u32[]{:S(2)}, u32[]{:S(2)}) %collective-permute-start.35) | collective-permute-done | bytes 32800 | tf_op jit(solution)/shard_map/ppermute | solution.py:65
  153.7 3.3 collective-permute-start.41
  160.5 3.4 collective-permute-start.43
  171.6 3.4 collective-permute-done.45
  175.0 3.9 collective-permute-start.46
  179.6 3.2 collective-permute-done.46
  182.9 5.8 %cholesky.59 = f32[64,64]{1,0:T(8,128)S(1)} custom-call(f32[64,64]{1,0:T(8,128)S(1)} %fusion.52), custom_call_target="Cholesky" | custom-call | tf_op jit(solution)/shard_map/jit(cholesky)/cholesky | solution.py:190
  190.0 4.9 %custom-call.7 = f32[1,64,64]{1,2,0:T(8,128)S(1)} custom-call(f32[1,64,64]{2,1,0:T(8,128)S(1)} %fusion.34), custom_call_target="InvertDiagBlocksLowerTriangular" | custom-call | tf_op jit(solution)/shard_map/jit(_solve_triangular)/triangular_solve | solution.py:191
  196.0 3.6 collective-permute-start.55
  203.9 2.6 constant_dynamic-slice_fusion.7
  221.8 2.3 collective-permute-done.57
  225.8 2.6 collective-permute-done.58
  228.5 3.0 collective-permute-start.59
  231.5 2.7 collective-permute-start.50
  234.2 5.6 %collective-permute-start.60 = (f32[128,64]{0,1:T(8,128)S(1)}, f32[128,64]{0,1:T(8,128)S(1)}, u32[]{:S(2)}, u32[]{:S(2)}) collective-permute-start(f32[128,64]{0,1:T(8,128)S(1)} %bitcast_add_fusion.19), channel_id=1, source_target_pairs={{0,0},{1,8},{2,16},{3,24},{4,32},{5,40},{6,48},{7,56},{8,64},{9,72... | collective-permute-start | bytes 98312 | tf_op jit(solution)/shard_map/ppermute | solution.py:62
  239.9 3.4 collective-permute-start.51
  244.2 3.5 collective-permute-done.51
  248.4 3.4 collective-permute-start.78
  251.8 4.1 collective-permute-start.61
  256.6 7.1 %collective-permute-done.61 = f32[128,64]{0,1:T(8,128)S(1)} collective-permute-done((f32[128,64]{0,1:T(8,128)S(1)}, f32[128,64]{0,1:T(8,128)S(1)}, u32[]{:S(2)}, u32[]{:S(2)}) %collective-permute-start.61) | collective-permute-done | bytes 32800 | tf_op jit(solution)/shard_map/ppermute | solution.py:65
  266.3 3.5 collective-permute-start.67
  275.0 3.5 collective-permute-done.69
  283.4 4.0 collective-permute-done.71
  287.4 5.5 %collective-permute-start.72 = (f32[96,64]{0,1:T(8,128)S(1)}, f32[96,64]{0,1:T(8,128)S(1)}, u32[]{:S(2)}, u32[]{:S(2)}) collective-permute-start(f32[96,64]{0,1:T(8,128)S(1)} %add.437), channel_id=1, source_target_pairs={{0,128},{1,129},{2,130},{3,131},{4,132},{5,133},{6,134},{7,135},{8... | collective-permute-start | bytes 73736 | tf_op jit(solution)/shard_map/ppermute | solution.py:102
  295.3 5.8 %cholesky.70 = f32[64,64]{1,0:T(8,128)S(1)} custom-call(f32[64,64]{1,0:T(8,128)S(1)} %fusion.47), custom_call_target="Cholesky" | custom-call | tf_op jit(solution)/shard_map/jit(cholesky)/cholesky | solution.py:190
  302.4 4.9 %custom-call.8 = f32[1,64,64]{1,2,0:T(8,128)S(1)} custom-call(f32[1,64,64]{2,1,0:T(8,128)S(1)} %fusion.35), custom_call_target="InvertDiagBlocksLowerTriangular" | custom-call | tf_op jit(solution)/shard_map/jit(_solve_triangular)/triangular_solve | solution.py:191
  314.6 2.6 constant_dynamic-slice_fusion.3
  336.9 3.1 collective-permute-done.84
  340.1 3.5 collective-permute-start.85
  345.6 7.1 %collective-permute-start.86 = (f32[128,64]{0,1:T(8,128)S(1)}, f32[128,64]{0,1:T(8,128)S(1)}, u32[]{:S(2)}, u32[]{:S(2)}) collective-permute-start(f32[128,64]{0,1:T(8,128)S(1)} %bitcast_add_fusion.16), channel_id=1, source_target_pairs={{0,0},{1,8},{2,16},{3,24},{4,32},{5,40},{6,48},{7,56},{8,64},{9,72... | collective-permute-start | bytes 98312 | tf_op jit(solution)/shard_map/ppermute | solution.py:62
  352.7 2.3 collective-permute-start.77
  355.7 5.0 %collective-permute-done.77 = f32[128,64]{0,1:T(8,128)S(1)} collective-permute-done((f32[128,64]{0,1:T(8,128)S(1)}, f32[128,64]{0,1:T(8,128)S(1)}, u32[]{:S(2)}, u32[]{:S(2)}) %collective-permute-start.77) | collective-permute-done | bytes 32800 | tf_op jit(solution)/shard_map/ppermute | solution.py:79
  361.0 3.9 collective-permute-done.87
  364.9 3.9 collective-permute-done.88
  369.6 4.6 %collective-permute-done.89 = f32[64,64]{0,1:T(8,128)S(1)} collective-permute-done((f32[64,64]{0,1:T(8,128)S(1)}, f32[64,64]{0,1:T(8,128)S(1)}, u32[]{:S(2)}, u32[]{:S(2)}) %collective-permute-start.89) | collective-permute-done | bytes 16416 | tf_op jit(solution)/shard_map/ppermute | solution.py:102
  375.9 5.0 %collective-permute-done.91 = f32[64,64]{0,1:T(8,128)S(1)} collective-permute-done((f32[64,64]{0,1:T(8,128)S(1)}, f32[64,64]{0,1:T(8,128)S(1)}, u32[]{:S(2)}, u32[]{:S(2)}) %collective-permute-start.91) | collective-permute-done | bytes 16416 | tf_op jit(solution)/shard_map/ppermute | solution.py:102
  381.2 3.9 collective-permute-done.92
  387.3 2.6 collective-permute-done.93
  389.9 2.8 collective-permute-start.94
  392.7 5.2 %collective-permute-done.94 = f32[64,64]{0,1:T(8,128)S(1)} collective-permute-done((f32[64,64]{0,1:T(8,128)S(1)}, f32[64,64]{0,1:T(8,128)S(1)}, u32[]{:S(2)}, u32[]{:S(2)}) %collective-permute-start.94) | collective-permute-done | bytes 16416 | tf_op jit(solution)/shard_map/ppermute | solution.py:102
  398.0 5.8 %cholesky.81 = f32[64,64]{1,0:T(8,128)S(1)} custom-call(f32[64,64]{1,0:T(8,128)S(1)} %fusion.42), custom_call_target="Cholesky" | custom-call | tf_op jit(solution)/shard_map/jit(cholesky)/cholesky | solution.py:190
  405.1 4.9 %custom-call.9 = f32[1,64,64]{1,2,0:T(8,128)S(1)} custom-call(f32[1,64,64]{2,1,0:T(8,128)S(1)} %fusion.36), custom_call_target="InvertDiagBlocksLowerTriangular" | custom-call | tf_op jit(solution)/shard_map/jit(_solve_triangular)/triangular_solve | solution.py:191
  (408 shorter events, 156.3 us)
Async XLA Ops:
  6.8 6.9 %collective-permute-start.1 = (f32[2,2,2,128,1]{3,2,1,0,4:T(2,128)S(1)}, f32[2,2,2,128,1]{3,2,1,0,4:T(2,128)S(1)}, u32[]{:S(2)}, u32[]{:S(2)}) collective-permute-start(f32[2,2,2,128,1]{3,2,1,0,4:T(2,128)S(1)} %bitcast.455), channel_id=1, source_target_pairs={{0,16},{8,24},{16,0},{24,8},{32,48},{40,56},{48,32},{56,40},{64,80... | collective-permute-start | bytes 12296 | tf_op jit(solution)/shard_map/ppermute | solution.py:79
  17.3 8.1 %collective-permute-start.3 = (f32[2,128,1]{1,2,0:T(1,128)S(1)}, f32[2,128,1]{1,2,0:T(1,128)S(1)}, u32[]{:S(2)}, u32[]{:S(2)}) collective-permute-start(f32[2,128,1]{1,2,0:T(1,128)S(1)} %fusion.85), channel_id=1, source_target_pairs={{0,64},{8,72},{16,80},{24,88},{32,96},{40,104},{48,112},{56,120},{... | collective-permute-start | bytes 3080 | tf_op jit(solution)/shard_map/ppermute | solution.py:79
  20.7 9.9 %collective-permute-start.8 = (f32[128,1]{0,1:T(1,128)S(1)}, f32[128,1]{0,1:T(1,128)S(1)}, u32[]{:S(2)}, u32[]{:S(2)}) collective-permute-start(f32[128,1]{0,1:T(1,128)S(1)} %fusion.91), channel_id=1, source_target_pairs={{0,0},{1,8},{2,16},{3,24},{4,32},{5,40},{6,48},{7,56},{8,64},{9,72... | collective-permute-start | bytes 1544 | tf_op jit(solution)/shard_map/ppermute | solution.py:62
  25.4 7.6 %collective-permute-start.4 = (f32[128,1]{0,1:T(1,128)S(1)}, f32[128,1]{0,1:T(1,128)S(1)}, u32[]{:S(2)}, u32[]{:S(2)}) collective-permute-start(f32[128,1]{0,1:T(1,128)S(1)} %fusion.89), channel_id=1, source_target_pairs={{0,128},{8,136},{16,144},{24,152},{32,160},{40,168},{48,176},{56,1... | collective-permute-start | bytes 1544 | tf_op jit(solution)/shard_map/ppermute | solution.py:79
  33.6 9.3 %collective-permute-start.18 = (f32[128,65]{0,1:T(8,128)S(1)}, f32[128,65]{0,1:T(8,128)S(1)}, u32[]{:S(2)}, u32[]{:S(2)}) collective-permute-start(f32[128,65]{0,1:T(8,128)S(1)} %pad_maximum_fusion.24), channel_id=1, source_target_pairs={{0,128},{8,136},{16,144},{24,152},{32,160},{40,168},{48,176},{56,1... | collective-permute-start | bytes 99848 | tf_op jit(solution)/shard_map/ppermute | solution.py:91
  38.6 10.7 %collective-permute-start.9 = (f32[128,65]{0,1:T(8,128)S(1)}, f32[128,65]{0,1:T(8,128)S(1)}, u32[]{:S(2)}, u32[]{:S(2)}) collective-permute-start(f32[128,65]{0,1:T(8,128)S(1)} %pad_maximum_fusion.24), channel_id=1, source_target_pairs={{0,0},{8,1},{16,2},{24,3},{32,4},{40,5},{48,6},{56,7},{64,8},{72,9... | collective-permute-start | bytes 99848 | tf_op jit(solution)/shard_map/ppermute | solution.py:65
  41.3 37.5 %collective-permute-start.27 = (f32[33,64]{1,0:T(8,128)S(1)}, f32[33,64]{1,0:T(8,128)S(1)}, u32[]{:S(2)}, u32[]{:S(2)}) collective-permute-start(f32[33,64]{1,0:T(8,128)S(1)} %concatenate.13), channel_id=1, source_target_pairs={{0,1},{1,0},{2,3},{3,2},{4,5},{5,4},{6,7},{7,6},{8,9},{9,8},{10,11... | collective-permute-start | bytes 25352 | tf_op jit(solution)/shard_map/ppermute | solution.py:102
  49.3 5.5 %collective-permute-start.10 = (f32[128,65]{0,1:T(8,128)S(1)}, f32[128,65]{0,1:T(8,128)S(1)}, u32[]{:S(2)}, u32[]{:S(2)}) collective-permute-start(f32[128,65]{0,1:T(8,128)S(1)} %collective-permute-done.9), channel_id=1, source_target_pairs={{0,4},{1,5},{2,6},{3,7},{4,0},{5,1},{6,2},{7,3},{8,12},{9,13},{10,... | collective-permute-start | bytes 99848 | tf_op jit(solution)/shard_map/ppermute | solution.py:91
  49.4 6.5 %collective-permute-start.19 = (f32[2,128,65]{1,0,2:T(2,128)S(1)}, f32[2,128,65]{1,0,2:T(2,128)S(1)}, u32[]{:S(2)}, u32[]{:S(2)}) collective-permute-start(f32[2,128,65]{1,0,2:T(2,128)S(1)} %pad_maximum_fusion.19), channel_id=1, source_target_pairs={{0,64},{8,72},{16,80},{24,88},{32,96},{40,104},{48,112},{56,120},{... | collective-permute-start | bytes 199688 | tf_op jit(solution)/shard_map/ppermute | solution.py:91
  59.3 8.8 %collective-permute-start.12 = (f32[2,2,128,65]{2,3,0,1:T(8,128)S(1)}, f32[2,2,128,65]{2,3,0,1:T(8,128)S(1)}, u32[]{:S(2)}, u32[]{:S(2)}) collective-permute-start(f32[2,2,128,65]{2,3,0,1:T(8,128)S(1)} %pad_maximum_fusion.12), channel_id=1, source_target_pairs={{0,1},{1,0},{2,3},{3,2},{4,5},{5,4},{6,7},{7,6},{8,9},{9,8},{10,11... | collective-permute-start | bytes 399368 | tf_op jit(solution)/shard_map/ppermute | solution.py:91
  62.1 13.6 %collective-permute-start.21 = (f32[2,2,2,128,65]{3,0,4,1,2:T(2,128)}, f32[2,2,2,128,65]{3,0,4,1,2:T(2,128)}, u32[]{:S(2)}, u32[]{:S(2)}) collective-permute-start(f32[2,2,2,128,65]{3,0,4,1,2:T(2,128)} %pad_maximum_fusion.7), channel_id=1, source_target_pairs={{0,16},{8,24},{16,0},{24,8},{32,48},{40,56},{48,32},{56,40},{64,80... | collective-permute-start | bytes 798728 | tf_op jit(solution)/shard_map/ppermute | solution.py:91
  75.7 9.5 %collective-permute-start.13 = (f32[2,2,2,2,128,64]{4,5,3,2,1,0:T(8,128)}, f32[2,2,2,2,128,64]{4,5,3,2,1,0:T(8,128)}, u32[]{:S(2)}, u32[]{:S(2)}) collective-permute-start(f32[2,2,2,2,128,64]{4,5,3,2,1,0:T(8,128)} %bitcast.421), channel_id=1, source_target_pairs={{0,8},{8,0},{16,24},{24,16},{32,40},{40,32},{48,56},{56,48},{64,72... | collective-permute-start | bytes 1572872 | tf_op jit(solution)/shard_map/ppermute | solution.py:79
  78.2 10.3 %collective-permute-start.22 = (f32[2,2,2,2,128,65]{4,3,5,2,1,0:T(2,128)}, f32[2,2,2,2,128,65]{4,3,5,2,1,0:T(2,128)}, u32[]{:S(2)}, u32[]{:S(2)}) collective-permute-start(f32[2,2,2,2,128,65]{4,3,5,2,1,0:T(2,128)} %copy.230), channel_id=1, source_target_pairs={{0,8},{8,0},{16,24},{24,16},{32,40},{40,32},{48,56},{56,48},{64,72... | collective-permute-start | bytes 1597448 | tf_op jit(solution)/shard_map/ppermute | solution.py:91
  83.3 15.7 %collective-permute-start.29 = (f32[33,64]{1,0:T(8,128)S(1)}, f32[33,64]{1,0:T(8,128)S(1)}, u32[]{:S(2)}, u32[]{:S(2)}) collective-permute-start(f32[33,64]{1,0:T(8,128)S(1)} %add.405), channel_id=1, source_target_pairs={{0,4},{1,5},{2,6},{3,7},{4,0},{5,1},{6,2},{7,3},{8,12},{9,13},{10,... | collective-permute-start | bytes 25352 | tf_op jit(solution)/shard_map/ppermute | solution.py:102
  87.3 10.6 %collective-permute-start.14 = (f32[2,2,2,128,64]{3,4,2,1,0:T(8,128)}, f32[2,2,2,128,64]{3,4,2,1,0:T(8,128)}, u32[]{:S(2)}, u32[]{:S(2)}) collective-permute-start(f32[2,2,2,128,64]{3,4,2,1,0:T(8,128)} %dynamic-slice_bitcast_fusion.2), channel_id=1, source_target_pairs={{0,16},{8,24},{16,0},{24,8},{32,48},{40,56},{48,32},{56,40},{64,80... | collective-permute-start | bytes 786440 | tf_op jit(solution)/shard_map/ppermute | solution.py:79
  97.0 5.1 %collective-permute-start.23 = (f32[2,2,128,64]{2,1,0,3:T(2,128)S(1)}, f32[2,2,128,64]{2,1,0,3:T(2,128)S(1)}, u32[]{:S(2)}, u32[]{:S(2)}) collective-permute-start(f32[2,2,128,64]{2,1,0,3:T(2,128)S(1)} %bitcast.442), channel_id=1, source_target_pairs={{0,1},{1,0},{2,3},{3,2},{4,5},{5,4},{6,7},{7,6},{8,9},{9,8},{10,11... | collective-permute-start | bytes 393224 | tf_op jit(solution)/shard_map/ppermute | solution.py:79
  100.3 18.6 %collective-permute-start.31 = (f32[33,64]{1,0:T(8,128)S(1)}, f32[33,64]{1,0:T(8,128)S(1)}, u32[]{:S(2)}, u32[]{:S(2)}) collective-permute-start(f32[33,64]{1,0:T(8,128)S(1)} %add.407), channel_id=1, source_target_pairs={{0,16},{1,17},{2,18},{3,19},{4,20},{5,21},{6,22},{7,23},{8,24},{9,... | collective-permute-start | bytes 25352 | tf_op jit(solution)/shard_map/ppermute | solution.py:102
  104.0 5.8 %collective-permute-start.16 = (f32[2,128,64]{1,2,0:T(8,128)S(1)}, f32[2,128,64]{1,2,0:T(8,128)S(1)}, u32[]{:S(2)}, u32[]{:S(2)}) collective-permute-start(f32[2,128,64]{1,2,0:T(8,128)S(1)} %dynamic-slice_bitcast_fusion.10), channel_id=1, source_target_pairs={{0,64},{8,72},{16,80},{24,88},{32,96},{40,104},{48,112},{56,120},{... | collective-permute-start | bytes 196616 | tf_op jit(solution)/shard_map/ppermute | solution.py:79
  106.7 5.5 %collective-permute-start.25 = (f32[128,64]{0,1:T(8,128)S(1)}, f32[128,64]{0,1:T(8,128)S(1)}, u32[]{:S(2)}, u32[]{:S(2)}) collective-permute-start(f32[128,64]{0,1:T(8,128)S(1)} %dynamic-slice_bitcast_fusion.15), channel_id=1, source_target_pairs={{0,4},{1,5},{2,6},{3,7},{4,0},{5,1},{6,2},{7,3},{8,12},{9,13},{10,... | collective-permute-start | bytes 98312 | tf_op jit(solution)/shard_map/ppermute | solution.py:79
  109.8 26.5 %collective-permute-start.17 = (f32[128,64]{0,1:T(8,128)S(1)}, f32[128,64]{0,1:T(8,128)S(1)}, u32[]{:S(2)}, u32[]{:S(2)}) collective-permute-start(f32[128,64]{0,1:T(8,128)S(1)} %dynamic-slice_bitcast_fusion.16), channel_id=1, source_target_pairs={{0,128},{8,136},{16,144},{24,152},{32,160},{40,168},{48,176},{56,1... | collective-permute-start | bytes 98312 | tf_op jit(solution)/shard_map/ppermute | solution.py:79
  112.2 24.1 %collective-permute-start.26 = (f32[128,64]{0,1:T(8,128)S(1)}, f32[128,64]{0,1:T(8,128)S(1)}, u32[]{:S(2)}, u32[]{:S(2)}) collective-permute-start(f32[128,64]{0,1:T(8,128)S(1)} %bitcast_add_fusion.22), channel_id=1, source_target_pairs={{0,0},{1,8},{2,16},{3,24},{4,32},{5,40},{6,48},{7,56},{8,64},{9,72... | collective-permute-start | bytes 98312 | tf_op jit(solution)/shard_map/ppermute | solution.py:62
  127.4 7.7 %collective-permute-start.34 = (f32[33,64]{1,0:T(8,128)S(1)}, f32[33,64]{1,0:T(8,128)S(1)}, u32[]{:S(2)}, u32[]{:S(2)}) collective-permute-start(f32[33,64]{1,0:T(8,128)S(1)} %add.410), channel_id=1, source_target_pairs={{0,128},{1,129},{2,130},{3,131},{4,132},{5,133},{6,134},{7,135},{8... | collective-permute-start | bytes 25352 | tf_op jit(solution)/shard_map/ppermute | solution.py:102
  137.2 6.1 %collective-permute-start.39 = (f32[96,64]{0,1:T(8,128)S(1)}, f32[96,64]{0,1:T(8,128)S(1)}, u32[]{:S(2)}, u32[]{:S(2)}) collective-permute-start(f32[96,64]{0,1:T(8,128)S(1)} %pad_maximum_fusion.25), channel_id=1, source_target_pairs={{0,1},{1,0},{2,3},{3,2},{4,5},{5,4},{6,7},{7,6},{8,9},{9,8},{10,11... | collective-permute-start | bytes 73736 | tf_op jit(solution)/shard_map/ppermute | solution.py:102
  137.4 7.9 %collective-permute-start.52 = (f32[128,64]{0,1:T(8,128)S(1)}, f32[128,64]{0,1:T(8,128)S(1)}, u32[]{:S(2)}, u32[]{:S(2)}) collective-permute-start(f32[128,64]{0,1:T(8,128)S(1)} %fusion.55), channel_id=1, source_target_pairs={{0,128},{8,136},{16,144},{24,152},{32,160},{40,168},{48,176},{56,1... | collective-permute-start | bytes 98312 | tf_op jit(solution)/shard_map/ppermute | solution.py:91
  141.4 10.5 %collective-permute-start.35 = (f32[128,64]{0,1:T(8,128)S(1)}, f32[128,64]{0,1:T(8,128)S(1)}, u32[]{:S(2)}, u32[]{:S(2)}) collective-permute-start(f32[128,64]{0,1:T(8,128)S(1)} %fusion.55), channel_id=1, source_target_pairs={{0,0},{8,1},{16,2},{24,3},{32,4},{40,5},{48,6},{56,7},{64,8},{72,9... | collective-permute-start | bytes 98312 | tf_op jit(solution)/shard_map/ppermute | solution.py:65
  143.4 10.4 %collective-permute-start.40 = (f32[96,64]{0,1:T(8,128)S(1)}, f32[96,64]{0,1:T(8,128)S(1)}, u32[]{:S(2)}, u32[]{:S(2)}) collective-permute-start(f32[96,64]{0,1:T(8,128)S(1)} %fusion.146), channel_id=1, source_target_pairs={{0,2},{1,3},{2,0},{3,1},{4,6},{5,7},{6,4},{7,5},{8,10},{9,11},{10,... | collective-permute-start | bytes 73736 | tf_op jit(solution)/shard_map/ppermute | solution.py:102
  151.9 5.4 %collective-permute-start.36 = (f32[128,64]{0,1:T(8,128)S(1)}, f32[128,64]{0,1:T(8,128)S(1)}, u32[]{:S(2)}, u32[]{:S(2)}) collective-permute-start(f32[128,64]{0,1:T(8,128)S(1)} %collective-permute-done.35), channel_id=1, source_target_pairs={{0,4},{1,5},{2,6},{3,7},{4,0},{5,1},{6,2},{7,3},{8,12},{9,13},{10,... | collective-permute-start | bytes 98312 | tf_op jit(solution)/shard_map/ppermute | solution.py:91
  151.9 11.9 %collective-permute-start.53 = (f32[2,128,64]{1,2,0:T(8,128)S(1)}, f32[2,128,64]{1,2,0:T(8,128)S(1)}, u32[]{:S(2)}, u32[]{:S(2)}) collective-permute-start(f32[2,128,64]{1,2,0:T(8,128)S(1)} %pad_maximum_fusion.21), channel_id=1, source_target_pairs={{0,64},{8,72},{16,80},{24,88},{32,96},{40,104},{48,112},{56,120},{... | collective-permute-start | bytes 196616 | tf_op jit(solution)/shard_map/ppermute | solution.py:91
  153.7 5.5 %collective-permute-start.41 = (f32[96,64]{0,1:T(8,128)S(1)}, f32[96,64]{0,1:T(8,128)S(1)}, u32[]{:S(2)}, u32[]{:S(2)}) collective-permute-start(f32[96,64]{0,1:T(8,128)S(1)} %add.414), channel_id=1, source_target_pairs={{0,4},{1,5},{2,6},{3,7},{4,0},{5,1},{6,2},{7,3},{8,12},{9,13},{10,... | collective-permute-start | bytes 73736 | tf_op jit(solution)/shard_map/ppermute | solution.py:102
  159.3 12.3 %collective-permute-start.37 = (f32[2,128,64]{1,2,0:T(8,128)S(1)}, f32[2,128,64]{1,2,0:T(8,128)S(1)}, u32[]{:S(2)}, u32[]{:S(2)}) collective-permute-start(f32[2,128,64]{1,2,0:T(8,128)S(1)} %pad_maximum_fusion.20), channel_id=1, source_target_pairs={{0,2},{1,3},{2,0},{3,1},{4,6},{5,7},{6,4},{7,5},{8,10},{9,11},{10,... | collective-permute-start | bytes 196616 | tf_op jit(solution)/shard_map/ppermute | solution.py:91
  160.5 5.4 %collective-permute-start.43 = (f32[96,64]{0,1:T(8,128)S(1)}, f32[96,64]{0,1:T(8,128)S(1)}, u32[]{:S(2)}, u32[]{:S(2)}) collective-permute-start(f32[96,64]{0,1:T(8,128)S(1)} %add.416), channel_id=1, source_target_pairs={{0,16},{1,17},{2,18},{3,19},{4,20},{5,21},{6,22},{7,23},{8,24},{9,... | collective-permute-start | bytes 73736 | tf_op jit(solution)/shard_map/ppermute | solution.py:102
  167.1 28.1 %collective-permute-start.54 = (f32[2,2,128,64]{2,3,0,1:T(8,128)S(1)}, f32[2,2,128,64]{2,3,0,1:T(8,128)S(1)}, u32[]{:S(2)}, u32[]{:S(2)}) collective-permute-start(f32[2,2,128,64]{2,3,0,1:T(8,128)S(1)} %pad_maximum_fusion.15), channel_id=1, source_target_pairs={{0,32},{8,40},{16,48},{24,56},{32,0},{40,8},{48,16},{56,24},{64,96... | collective-permute-start | bytes 393224 | tf_op jit(solution)/shard_map/ppermute | solution.py:91
  175.0 7.8 %collective-permute-start.46 = (f32[96,64]{0,1:T(8,128)S(1)}, f32[96,64]{0,1:T(8,128)S(1)}, u32[]{:S(2)}, u32[]{:S(2)}) collective-permute-start(f32[96,64]{0,1:T(8,128)S(1)} %add.419), channel_id=1, source_target_pairs={{0,128},{1,129},{2,130},{3,131},{4,132},{5,133},{6,134},{7,135},{8... | collective-permute-start | bytes 73736 | tf_op jit(solution)/shard_map/ppermute | solution.py:102
  178.9 20.6 %collective-permute-start.38 = (f32[2,2,128,64]{2,3,0,1:T(8,128)S(1)}, f32[2,2,128,64]{2,3,0,1:T(8,128)S(1)}, u32[]{:S(2)}, u32[]{:S(2)}) collective-permute-start(f32[2,2,128,64]{2,3,0,1:T(8,128)S(1)} %pad_maximum_fusion.14), channel_id=1, source_target_pairs={{0,1},{1,0},{2,3},{3,2},{4,5},{5,4},{6,7},{7,6},{8,9},{9,8},{10,11... | collective-permute-start | bytes 393224 | tf_op jit(solution)/shard_map/ppermute | solution.py:91
  196.0 10.8 %collective-permute-start.55 = (f32[2,2,2,128,64]{3,4,0,1,2:T(8,128)}, f32[2,2,2,128,64]{3,4,0,1,2:T(8,128)}, u32[]{:S(2)}, u32[]{:S(2)}) collective-permute-start(f32[2,2,2,128,64]{3,4,0,1,2:T(8,128)} %pad_maximum_fusion.9), channel_id=1, source_target_pairs={{0,16},{8,24},{16,0},{24,8},{32,48},{40,56},{48,32},{56,40},{64,80... | collective-permute-start | bytes 786440 | tf_op jit(solution)/shard_map/ppermute | solution.py:91
  209.8 10.0 %collective-permute-start.48 = (f32[2,2,2,128,64]{3,4,2,1,0:T(8,128)S(1)}, f32[2,2,2,128,64]{3,4,2,1,0:T(8,128)}, u32[]{:S(2)}, u32[]{:S(2)}) collective-permute-start(f32[2,2,2,128,64]{3,4,2,1,0:T(8,128)S(1)} %dynamic-slice_bitcast_fusion.1), channel_id=1, source_target_pairs={{0,16},{8,24},{16,0},{24,8},{32,48},{40,56},{48,32},{56,40},{64,80... | collective-permute-start | bytes 786440 | tf_op jit(solution)/shard_map/ppermute | solution.py:79
  218.2 5.9 %collective-permute-start.57 = (f32[2,2,128,64]{2,3,1,0:T(8,128)S(1)}, f32[2,2,128,64]{2,3,1,0:T(8,128)S(1)}, u32[]{:S(2)}, u32[]{:S(2)}) collective-permute-start(f32[2,2,128,64]{2,3,1,0:T(8,128)S(1)} %bitcast.439), channel_id=1, source_target_pairs={{0,1},{1,0},{2,3},{3,2},{4,5},{5,4},{6,7},{7,6},{8,9},{9,8},{10,11... | collective-permute-start | bytes 393224 | tf_op jit(solution)/shard_map/ppermute | solution.py:79
  228.5 5.7 %collective-permute-start.59 = (f32[128,64]{0,1:T(8,128)S(1)}, f32[128,64]{0,1:T(8,128)S(1)}, u32[]{:S(2)}, u32[]{:S(2)}) collective-permute-start(f32[128,64]{0,1:T(8,128)S(1)} %dynamic-slice_bitcast_fusion.13), channel_id=1, source_target_pairs={{0,4},{1,5},{2,6},{3,7},{4,0},{5,1},{6,2},{7,3},{8,12},{9,13},{10,... | collective-permute-start | bytes 98312 | tf_op jit(solution)/shard_map/ppermute | solution.py:79
  231.5 8.3 %collective-permute-start.50 = (f32[2,128,64]{1,2,0:T(8,128)S(1)}, f32[2,128,64]{1,2,0:T(8,128)S(1)}, u32[]{:S(2)}, u32[]{:S(2)}) collective-permute-start(f32[2,128,64]{1,2,0:T(8,128)S(1)} %dynamic-slice_bitcast_fusion.9), channel_id=1, source_target_pairs={{0,64},{8,72},{16,80},{24,88},{32,96},{40,104},{48,112},{56,120},{... | collective-permute-start | bytes 196616 | tf_op jit(solution)/shard_map/ppermute | solution.py:79
  234.2 10.0 %collective-permute-start.60 = (f32[128,64]{0,1:T(8,128)S(1)}, f32[128,64]{0,1:T(8,128)S(1)}, u32[]{:S(2)}, u32[]{:S(2)}) collective-permute-start(f32[128,64]{0,1:T(8,128)S(1)} %bitcast_add_fusion.19), channel_id=1, source_target_pairs={{0,0},{1,8},{2,16},{3,24},{4,32},{5,40},{6,48},{7,56},{8,64},{9,72... | collective-permute-start | bytes 98312 | tf_op jit(solution)/shard_map/ppermute | solution.py:62
  239.9 7.9 %collective-permute-start.51 = (f32[128,64]{0,1:T(8,128)S(1)}, f32[128,64]{0,1:T(8,128)S(1)}, u32[]{:S(2)}, u32[]{:S(2)}) collective-permute-start(f32[128,64]{0,1:T(8,128)S(1)} %dynamic-slice_bitcast_fusion.14), channel_id=1, source_target_pairs={{0,128},{8,136},{16,144},{24,152},{32,160},{40,168},{48,176},{56,1... | collective-permute-start | bytes 98312 | tf_op jit(solution)/shard_map/ppermute | solution.py:79
  248.3 7.6 %collective-permute-start.65 = (f32[96,64]{0,1:T(8,128)S(1)}, f32[96,64]{0,1:T(8,128)S(1)}, u32[]{:S(2)}, u32[]{:S(2)}) collective-permute-start(f32[96,64]{0,1:T(8,128)S(1)} %pad_maximum_fusion.26), channel_id=1, source_target_pairs={{0,1},{1,0},{2,3},{3,2},{4,5},{5,4},{6,7},{7,6},{8,9},{9,8},{10,11... | collective-permute-start | bytes 73736 | tf_op jit(solution)/shard_map/ppermute | solution.py:102
  248.4 8.2 %collective-permute-start.78 = (f32[128,64]{0,1:T(8,128)S(1)}, f32[128,64]{0,1:T(8,128)S(1)}, u32[]{:S(2)}, u32[]{:S(2)}) collective-permute-start(f32[128,64]{0,1:T(8,128)S(1)} %fusion.50), channel_id=1, source_target_pairs={{0,128},{8,136},{16,144},{24,152},{32,160},{40,168},{48,176},{56,1... | collective-permute-start | bytes 98312 | tf_op jit(solution)/shard_map/ppermute | solution.py:91
  251.8 11.9 %collective-permute-start.61 = (f32[128,64]{0,1:T(8,128)S(1)}, f32[128,64]{0,1:T(8,128)S(1)}, u32[]{:S(2)}, u32[]{:S(2)}) collective-permute-start(f32[128,64]{0,1:T(8,128)S(1)} %fusion.50), channel_id=1, source_target_pairs={{0,0},{8,1},{16,2},{24,3},{32,4},{40,5},{48,6},{56,7},{64,8},{72,9... | collective-permute-start | bytes 98312 | tf_op jit(solution)/shard_map/ppermute | solution.py:65
  256.0 10.3 %collective-permute-start.66 = (f32[96,64]{0,1:T(8,128)S(1)}, f32[96,64]{0,1:T(8,128)S(1)}, u32[]{:S(2)}, u32[]{:S(2)}) collective-permute-start(f32[96,64]{0,1:T(8,128)S(1)} %fusion.145), channel_id=1, source_target_pairs={{0,2},{1,3},{2,0},{3,1},{4,6},{5,7},{6,4},{7,5},{8,10},{9,11},{10,... | collective-permute-start | bytes 73736 | tf_op jit(solution)/shard_map/ppermute | solution.py:102
  263.7 6.1 %collective-permute-start.62 = (f32[128,64]{0,1:T(8,128)S(1)}, f32[128,64]{0,1:T(8,128)S(1)}, u32[]{:S(2)}, u32[]{:S(2)}) collective-permute-start(f32[128,64]{0,1:T(8,128)S(1)} %collective-permute-done.61), channel_id=1, source_target_pairs={{0,4},{1,5},{2,6},{3,7},{4,0},{5,1},{6,2},{7,3},{8,12},{9,13},{10,... | collective-permute-start | bytes 98312 | tf_op jit(solution)/shard_map/ppermute | solution.py:91
  264.3 10.6 %collective-permute-start.79 = (f32[2,128,64]{1,2,0:T(8,128)S(1)}, f32[2,128,64]{1,2,0:T(8,128)S(1)}, u32[]{:S(2)}, u32[]{:S(2)}) collective-permute-start(f32[2,128,64]{1,2,0:T(8,128)S(1)} %pad_maximum_fusion.23), channel_id=1, source_target_pairs={{0,64},{8,72},{16,80},{24,88},{32,96},{40,104},{48,112},{56,120},{... | collective-permute-start | bytes 196616 | tf_op jit(solution)/shard_map/ppermute | solution.py:91
  266.3 5.5 %collective-permute-start.67 = (f32[96,64]{0,1:T(8,128)S(1)}, f32[96,64]{0,1:T(8,128)S(1)}, u32[]{:S(2)}, u32[]{:S(2)}) collective-permute-start(f32[96,64]{0,1:T(8,128)S(1)} %add.432), channel_id=1, source_target_pairs={{0,4},{1,5},{2,6},{3,7},{4,0},{5,1},{6,2},{7,3},{8,12},{9,13},{10,... | collective-permute-start | bytes 73736 | tf_op jit(solution)/shard_map/ppermute | solution.py:102
  271.8 11.5 %collective-permute-start.63 = (f32[2,128,64]{1,2,0:T(8,128)S(1)}, f32[2,128,64]{1,2,0:T(8,128)S(1)}, u32[]{:S(2)}, u32[]{:S(2)}) collective-permute-start(f32[2,128,64]{1,2,0:T(8,128)S(1)} %pad_maximum_fusion.22), channel_id=1, source_target_pairs={{0,2},{1,3},{2,0},{3,1},{4,6},{5,7},{6,4},{7,5},{8,10},{9,11},{10,... | collective-permute-start | bytes 196616 | tf_op jit(solution)/shard_map/ppermute | solution.py:91
  273.0 5.4 %collective-permute-start.69 = (f32[96,64]{0,1:T(8,128)S(1)}, f32[96,64]{0,1:T(8,128)S(1)}, u32[]{:S(2)}, u32[]{:S(2)}) collective-permute-start(f32[96,64]{0,1:T(8,128)S(1)} %add.434), channel_id=1, source_target_pairs={{0,16},{1,17},{2,18},{3,19},{4,20},{5,21},{6,22},{7,23},{8,24},{9,... | collective-permute-start | bytes 73736 | tf_op jit(solution)/shard_map/ppermute | solution.py:102
  279.4 28.2 %collective-permute-start.80 = (f32[2,2,128,64]{2,3,0,1:T(8,128)S(1)}, f32[2,2,128,64]{2,3,0,1:T(8,128)S(1)}, u32[]{:S(2)}, u32[]{:S(2)}) collective-permute-start(f32[2,2,128,64]{2,3,0,1:T(8,128)S(1)} %pad_maximum_fusion.17), channel_id=1, source_target_pairs={{0,32},{8,40},{16,48},{24,56},{32,0},{40,8},{48,16},{56,24},{64,96... | collective-permute-start | bytes 393224 | tf_op jit(solution)/shard_map/ppermute | solution.py:91
  287.4 7.8 %collective-permute-start.72 = (f32[96,64]{0,1:T(8,128)S(1)}, f32[96,64]{0,1:T(8,128)S(1)}, u32[]{:S(2)}, u32[]{:S(2)}) collective-permute-start(f32[96,64]{0,1:T(8,128)S(1)} %add.437), channel_id=1, source_target_pairs={{0,128},{1,129},{2,130},{3,131},{4,132},{5,133},{6,134},{7,135},{8... | collective-permute-start | bytes 73736 | tf_op jit(solution)/shard_map/ppermute | solution.py:102
  292.9 17.3 %collective-permute-start.64 = (f32[2,2,128,64]{2,3,0,1:T(8,128)S(1)}, f32[2,2,128,64]{2,3,0,1:T(8,128)S(1)}, u32[]{:S(2)}, u32[]{:S(2)}) collective-permute-start(f32[2,2,128,64]{2,3,0,1:T(8,128)S(1)} %pad_maximum_fusion.16), channel_id=1, source_target_pairs={{0,1},{1,0},{2,3},{3,2},{4,5},{5,4},{6,7},{7,6},{8,9},{9,8},{10,11... | collective-permute-start | bytes 393224 | tf_op jit(solution)/shard_map/ppermute | solution.py:91
  308.4 9.1 %collective-permute-start.81 = (f32[2,2,2,128,64]{3,4,0,1,2:T(8,128)}, f32[2,2,2,128,64]{3,4,0,1,2:T(8,128)}, u32[]{:S(2)}, u32[]{:S(2)}) collective-permute-start(f32[2,2,2,128,64]{3,4,0,1,2:T(8,128)} %pad_maximum_fusion.11), channel_id=1, source_target_pairs={{0,16},{8,24},{16,0},{24,8},{32,48},{40,56},{48,32},{56,40},{64,80... | collective-permute-start | bytes 786440 | tf_op jit(solution)/shard_map/ppermute | solution.py:91
  320.4 10.2 %collective-permute-start.74 = (f32[2,2,2,128,64]{3,4,2,1,0:T(8,128)S(1)}, f32[2,2,2,128,64]{3,4,2,1,0:T(8,128)}, u32[]{:S(2)}, u32[]{:S(2)}) collective-permute-start(f32[2,2,2,128,64]{3,4,2,1,0:T(8,128)S(1)} %dynamic-slice_bitcast_fusion), channel_id=1, source_target_pairs={{0,16},{8,24},{16,0},{24,8},{32,48},{40,56},{48,32},{56,40},{64,80... | collective-permute-start | bytes 786440 | tf_op jit(solution)/shard_map/ppermute | solution.py:79
  330.3 5.3 %collective-permute-start.83 = (f32[2,2,128,64]{2,3,1,0:T(8,128)S(1)}, f32[2,2,128,64]{2,3,1,0:T(8,128)S(1)}, u32[]{:S(2)}, u32[]{:S(2)}) collective-permute-start(f32[2,2,128,64]{2,3,1,0:T(8,128)S(1)} %bitcast.438), channel_id=1, source_target_pairs={{0,1},{1,0},{2,3},{3,2},{4,5},{5,4},{6,7},{7,6},{8,9},{9,8},{10,11... | collective-permute-start | bytes 393224 | tf_op jit(solution)/shard_map/ppermute | solution.py:79
  331.7 5.2 %collective-permute-start.75 = (f32[2,2,128,64]{2,3,1,0:T(8,128)S(1)}, f32[2,2,128,64]{2,3,1,0:T(8,128)S(1)}, u32[]{:S(2)}, u32[]{:S(2)}) collective-permute-start(f32[2,2,128,64]{2,3,1,0:T(8,128)S(1)} %dynamic-slice_bitcast_fusion.3), channel_id=1, source_target_pairs={{0,32},{8,40},{16,48},{24,56},{32,0},{40,8},{48,16},{56,24},{64,96... | collective-permute-start | bytes 393224 | tf_op jit(solution)/shard_map/ppermute | solution.py:79
  340.1 5.5 %collective-permute-start.85 = (f32[128,64]{0,1:T(8,128)S(1)}, f32[128,64]{0,1:T(8,128)S(1)}, u32[]{:S(2)}, u32[]{:S(2)}) collective-permute-start(f32[128,64]{0,1:T(8,128)S(1)} %dynamic-slice_bitcast_fusion.11), channel_id=1, source_target_pairs={{0,4},{1,5},{2,6},{3,7},{4,0},{5,1},{6,2},{7,3},{8,12},{9,13},{10,... | collective-permute-start | bytes 98312 | tf_op jit(solution)/shard_map/ppermute | solution.py:79
  343.5 9.1 %collective-permute-start.76 = (f32[2,128,64]{1,2,0:T(8,128)S(1)}, f32[2,128,64]{1,2,0:T(8,128)S(1)}, u32[]{:S(2)}, u32[]{:S(2)}) collective-permute-start(f32[2,128,64]{1,2,0:T(8,128)S(1)} %dynamic-slice_bitcast_fusion.7), channel_id=1, source_target_pairs={{0,64},{8,72},{16,80},{24,88},{32,96},{40,104},{48,112},{56,120},{... | collective-permute-start | bytes 196616 | tf_op jit(solution)/shard_map/ppermute | solution.py:79
  345.6 10.1 %collective-permute-start.86 = (f32[128,64]{0,1:T(8,128)S(1)}, f32[128,64]{0,1:T(8,128)S(1)}, u32[]{:S(2)}, u32[]{:S(2)}) collective-permute-start(f32[128,64]{0,1:T(8,128)S(1)} %bitcast_add_fusion.16), channel_id=1, source_target_pairs={{0,0},{1,8},{2,16},{3,24},{4,32},{5,40},{6,48},{7,56},{8,64},{9,72... | collective-permute-start | bytes 98312 | tf_op jit(solution)/shard_map/ppermute | solution.py:62
  352.7 8.0 %collective-permute-start.77 = (f32[128,64]{0,1:T(8,128)S(1)}, f32[128,64]{0,1:T(8,128)S(1)}, u32[]{:S(2)}, u32[]{:S(2)}) collective-permute-start(f32[128,64]{0,1:T(8,128)S(1)} %dynamic-slice_bitcast_fusion.12), channel_id=1, source_target_pairs={{0,128},{8,136},{16,144},{24,152},{32,160},{40,168},{48,176},{56,1... | collective-permute-start | bytes 98312 | tf_op jit(solution)/shard_map/ppermute | solution.py:79
  368.9 5.4 %collective-permute-start.89 = (f32[64,64]{0,1:T(8,128)S(1)}, f32[64,64]{0,1:T(8,128)S(1)}, u32[]{:S(2)}, u32[]{:S(2)}) collective-permute-start(f32[64,64]{0,1:T(8,128)S(1)} %add.450), channel_id=1, source_target_pairs={{0,4},{1,5},{2,6},{3,7},{4,0},{5,1},{6,2},{7,3},{8,12},{9,13},{10,... | collective-permute-start | bytes 49160 | tf_op jit(solution)/shard_map/ppermute | solution.py:102
  375.5 5.4 %collective-permute-start.91 = (f32[64,64]{0,1:T(8,128)S(1)}, f32[64,64]{0,1:T(8,128)S(1)}, u32[]{:S(2)}, u32[]{:S(2)}) collective-permute-start(f32[64,64]{0,1:T(8,128)S(1)} %add.452), channel_id=1, source_target_pairs={{0,16},{1,17},{2,18},{3,19},{4,20},{5,21},{6,22},{7,23},{8,24},{9,... | collective-permute-start | bytes 49160 | tf_op jit(solution)/shard_map/ppermute | solution.py:102
  389.9 7.9 %collective-permute-start.94 = (f32[64,64]{0,1:T(8,128)S(1)}, f32[64,64]{0,1:T(8,128)S(1)}, u32[]{:S(2)}, u32[]{:S(2)}) collective-permute-start(f32[64,64]{0,1:T(8,128)S(1)} %add.455), channel_id=1, source_target_pairs={{0,128},{1,129},{2,130},{3,131},{4,132},{5,133},{6,134},{7,135},{8... | collective-permute-start | bytes 49160 | tf_op jit(solution)/shard_map/ppermute | solution.py:102
  (42 other events, 177.0 us)
